TPU v7x, 128 devices: a whole 4x4x4 slice. The times are simulated.
128 devices in a mesh: amp: 16 (over x_hi, z, core), int: 8 (over x_lo, y).
Axes of the slice: x: 4 (x_hi: 2, x_lo: 2; x = x_hi * 2 + x_lo), y: 4, z: 4, core: 2. Of those that a mesh axis runs over, the one named last changes fastest.
Arguments:
- amplitudes: bfloat16 [1024, 384, 768], P('amp', None, 'int'), may hold values from -6 to 6
- integrals: bfloat16 [384, 768, 1536], P('amp', 'int'), may hold values from -0.015625 to 0.015625
- rest_residual: float32 [1024, 1536], P('amp', 'int'), may hold values from -6 to 6
- old_amplitudes: float32 [1024, 1536], P('amp', 'int'), may hold values from -3 to 3
- pair_energy: float32 [1024], P('amp'), may hold values from -4 to -1
- virt_energy: float32 [1536], P('int'), may hold values from 0.4 to 6
Outputs:
- new_amplitudes: float32 [1024, 1536], P('amp', 'int')
All inputs are finite; a program needn't handle non-finite values.
Results may differ from a plain program's by a relative error of at most 0.0003.
Values may be sent and summed in bfloat16 or wider, within the bound.
No kernel may reach another device: no remote copies, remote signals or barrier semaphores. Data moves between devices by JAX's collectives and lax.ppermute only.
A program may use at most 128 MiB of HBM per device.

v0:
```python
import jax
import jax.numpy as jnp
from jax import lax
from jax.sharding import PartitionSpec as P


def local(amplitudes, integrals, rest_residual, old_amplitudes, pair_energy, virt_energy):
    regrouped = lax.all_to_all(amplitudes, "amp", split_axis=1, concat_axis=0, tiled=True)
    partial_rows = lax.psum_scatter(
        lax.dot_general(
            regrouped, integrals, (((1, 2), (0, 1)), ((), ())), preferred_element_type=jnp.float32
        ),
        "amp",
        scatter_dimension=0,
        tiled=True,
    )
    ladder = lax.psum_scatter(partial_rows, "int", scatter_dimension=1, tiled=True)
    denominator = pair_energy[:, None] - virt_energy[None, :]
    return 0.4 * old_amplitudes + 0.6 * (ladder + rest_residual) / denominator


def solution(mesh):
    placed = (
        P("amp", None, "int"),
        P("amp", "int", None),
        P("amp", "int"),
        P("amp", "int"),
        P("amp"),
        P("int"),
    )
    return jax.shard_map(
        local, mesh=mesh, in_specs=placed, out_specs=P("amp", "int"), check_vma=False
    )
```

profile of v0, /device:TPU:0, one launch (start us, length us, event | category | flops | bytes accessed | tf_op | source)
XLA Modules:
  0.0 251.6 jit_solution(5609339371970099490)
XLA Ops:
  6.5 0.0 reduce-scatter.5.cloned.1.call-start
  6.5 8.7 %copy.11 = bf16[64,384,96]{2,0,1:T(8,128)(2,1)} copy(bf16[64,384,96]{1,2,0:T(8,128)(2,1)} %param.6) | data formatting | bytes 9437184 | tf_op args[0]
  15.2 82.1 %all_to_all.18 = bf16[64,384,96]{2,0,1:T(8,128)(2,1)S(1)} all-to-all(bf16[64,384,96]{2,0,1:T(8,128)(2,1)} %copy.11), channel_id=1, replica_groups=mesh['amp'=16,'int'=8] {'amp'}, dimensions={1} | all-to-all | bytes 9437184 | tf_op jit(solution)/shard_map/all_to_all | solution.py:8
  97.3 5.3 %copy.13 = bf16[16,64,24,96]{3,2,1,0:T(8,128)(2,1)S(1)} copy(bf16[16,64,24,96]{3,1,2,0:T(8,128)(2,1)S(1)} %bitcast.9) | data formatting | bytes 9437184 | tf_op jit(solution)/shard_map/all_to_all | solution.py:8
  102.6 13.5 %fusion.2 = f32[1024,1536]{1,0:T(8,128)} fusion(bf16[24,96,1536]{2,1,0:T(8,128)(2,1)} %param.7, bf16[1024,24,96]{2,1,0:T(8,128)(2,1)S(1)} %bitcast.10), kind=kOutput, calls=%fused_computation.2 | convolution fusion | flops 7247757312 | bytes 18087936 | tf_op jit(solution)/shard_map/dot_general | solution.py:10
  116.1 0.0 copy-start
  116.1 0.0 copy-start.1
  116.1 0.0 copy-start.2
  116.1 0.0 copy-start.3
  116.1 0.0 reduce-scatter.5.cloned.1.call-update
  116.1 0.0 reduce-scatter.7.cloned.1.call-start
  116.2 87.2 %reduce-scatter.5.cloned.1.call-done = f32[64,1536]{1,0:T(8,128)} async-done(((f32[1024,1536]{1,0:T(8,128)}), f32[64,1536]{1,0:T(8,128)}) %reduce-scatter.5.cloned.1.call-update) | async-done | bytes 393232 | tf_op jit(solution)/shard_map/reduce_scatter | solution.py:9
  203.4 2.2 copy.16
  205.5 0.0 reduce-scatter.7.cloned.1.call-update
  205.6 37.5 %reduce-scatter.7.cloned.1.call-done = f32[192,64]{1,0:T(8,128)} async-done(((f32[1536,64]{1,0:T(8,128)}), f32[192,64]{1,0:T(8,128)}) %reduce-scatter.7.cloned.1.call-update) | async-done | bytes 49168
  243.1 1.0 copy.17
  244.0 0.0 copy-done
  244.0 0.0 copy-done.1
  244.1 0.0 copy-done.2
  244.1 0.0 copy-done.3
  244.1 0.7 divide_add_fusion
Async XLA Ops:
  6.5 196.9 %reduce-scatter.5.cloned.1.call-start = ((), (), s32[]{:S(2)}) async-start(), calls=%async_computation.3 | async-start | bytes 6684672 | tf_op jit(solution)/shard_map/reduce_scatter | solution.py:9
  116.1 127.9 %copy-start = (f32[64,192]{1,0:T(8,128)S(1)}, f32[64,192]{1,0:T(8,128)}, u32[]{:S(2)}) copy-start(f32[64,192]{1,0:T(8,128)} %param.8) | copy-start | bytes 147460
  116.1 128.0 %copy-start.1 = (f32[64,192]{1,0:T(8,128)S(1)}, f32[64,192]{1,0:T(8,128)}, u32[]{:S(2)}) copy-start(f32[64,192]{1,0:T(8,128)} %param.9) | copy-start | bytes 147460
  116.1 128.0 %copy-start.2 = (f32[192]{0:T(256)S(1)}, f32[192]{0:T(256)}, u32[]{:S(2)}) copy-start(f32[192]{0:T(256)} %param.11) | copy-start | bytes 2308
  116.1 128.0 %copy-start.3 = (f32[64]{0:T(128)S(1)}, f32[64]{0:T(128)}, u32[]{:S(2)}) copy-start(f32[64]{0:T(128)} %param.10) | copy-start | bytes 772
  116.1 126.9 %reduce-scatter.7.cloned.1.call-start = ((), (), s32[]{:S(2)}) async-start(), calls=%async_computation.4 | async-start | bytes 884736
Sparse Core Ops, SparseCore 0:
  116.3 87.0 reduce-scatter.4
  205.9 37.1 reduce-scatter.6
where the time goes:
time: 252 us
  waiting for transfers between devices  125 us (50%)
  blocking collectives  82.1 us (33%)
  local copies, waits for them, and re-layouts  17.1 us (7%)
  matrix products  13.5 us (5%)
  between operations  13.5 us (5%)
    reduce_scatter x1, waiting for transfers between devices, local(): lax.psum_scatter(lax.dot_general(regrouped, integrals, (((1, 2), (0, 1)),...  87.2 us
    all_to_all x1, blocking collectives, local(): lax.all_to_all(amplitudes, 'amp', split_axis=1, concat_axis=0, tiled=True)  82.1 us
    unnamed x3, waiting for transfers between devices  37.5 us
    dot_general x1, matrix products, local(): lax.dot_general(regrouped, integrals, (((1, 2), (0, 1)), ((), ())), prefe...  13.5 us
    unnamed x11, local copies, waits for them, and re-layouts  11.8 us
    all_to_all x1, local copies, waits for them, and re-layouts, local(): lax.all_to_all(amplitudes, 'amp', split_axis=1, concat_axis=0, tiled=True)  5.27 us
  transfers between devices with their start and end apart: 2, of which 2 were waited for; matrix products, arithmetic and copies ran while one was open for 0% of the time, Pallas kernels for 0%

commit v1 on v0

v1 whole, which is shorter than its diff:
```python
import jax
import jax.numpy as jnp
from jax import lax
from jax.sharding import PartitionSpec as P


def scatter_sum(x, axis_name, axis):
    n = lax.axis_size(axis_name)
    me = lax.axis_index(axis_name)
    width = x.shape[axis] // n
    total = lax.dynamic_slice_in_dim(x, me * width, width, axis=axis)
    for s in range(1, n):
        block = lax.dynamic_slice_in_dim(x, ((me + s) % n) * width, width, axis=axis)
        total = total + lax.ppermute(block, axis_name, [(i, (i + s) % n) for i in range(n)])
    return total


def local(amplitudes, integrals, rest_residual, old_amplitudes, pair_energy, virt_energy):
    regrouped = lax.all_to_all(amplitudes, "amp", split_axis=1, concat_axis=0, tiled=True)
    partial = lax.dot_general(
        regrouped, integrals, (((1, 2), (0, 1)), ((), ())), preferred_element_type=jnp.float32
    )
    rows = lax.psum_scatter(partial, "amp", scatter_dimension=0, tiled=True)
    ladder = scatter_sum(rows, "int", 1)
    denominator = pair_energy[:, None] - virt_energy[None, :]
    return 0.4 * old_amplitudes + 0.6 * (ladder + rest_residual) / denominator


def solution(mesh):
    placed = (
        P("amp", None, "int"),
        P("amp", "int", None),
        P("amp", "int"),
        P("amp", "int"),
        P("amp"),
        P("int"),
    )
    return jax.shard_map(
        local, mesh=mesh, in_specs=placed, out_specs=P("amp", "int"), check_vma=False
    )
```

time: 252 us -> 231 us (0.917)
  waiting for transfers between devices: 125 us -> 93.5 us
  starting transfers between devices: 0.04 us -> 10.8 us
    unnamed x3 -> x1, waiting for transfers between devices: 37.5 us -> 0.02 us
    ppermute x0 -> x7, starting transfers between devices: none -> 10.8 us  [scatter_sum(): lax.ppermute(block, axis_name, [(i, (i + s) % n) for i in range(n)])]
    ppermute x0 -> x7, waiting for transfers between devices: none -> 6.29 us  [scatter_sum(): lax.ppermute(block, axis_name, [(i, (i + s) % n) for i in range(n)])]
    unnamed x11 -> x9, local copies, waits for them, and re-layouts: 11.8 us -> 8.66 us
  transfers between devices with their start and end apart: 2 -> 8, of which waited for: 2 -> 4; matrix products, arithmetic and copies ran while one was open for 0% -> 0% of each run, Pallas kernels for 0% -> 0%
where the time goes in v1:
time: 231 us; the launch traced here: 230 us
  waiting for transfers between devices  93.5 us (40%)
  blocking collectives  82.1 us (36%)
  local copies, waits for them, and re-layouts  15.3 us (7%)
  matrix products  13.5 us (6%)
  between operations  13.5 us (6%)
  starting transfers between devices  10.8 us (5%)
    reduce_scatter x1, waiting for transfers between devices, local(): rows = lax.psum_scatter(partial, 'amp', scatter_dimension=0, tiled=True)  87.2 us
    all_to_all x1, blocking collectives, local(): lax.all_to_all(amplitudes, 'amp', split_axis=1, concat_axis=0, tiled=True)  82.1 us
    dot_general x1, matrix products, local(): lax.dot_general(regrouped, integrals, (((1, 2), (0, 1)), ((), ())), prefe...  13.5 us
    ppermute x7, starting transfers between devices, scatter_sum(): lax.ppermute(block, axis_name, [(i, (i + s) % n) for i in range(n)])  10.8 us
    unnamed x9, local copies, waits for them, and re-layouts  8.66 us
    ppermute x7, waiting for transfers between devices, scatter_sum(): lax.ppermute(block, axis_name, [(i, (i + s) % n) for i in range(n)])  6.29 us
    all_to_all x1, local copies, waits for them, and re-layouts, local(): lax.all_to_all(amplitudes, 'amp', split_axis=1, concat_axis=0, tiled=True)  5.27 us
  transfers between devices with their start and end apart: 8, of which 4 were waited for; matrix products, arithmetic and copies ran while one was open for 0% of the time, Pallas kernels for 0%

profile of v1, /device:TPU:0, one launch (start us, length us, event | category | flops | bytes accessed | tf_op | source)
XLA Modules:
  0.0 230.4 jit_solution(9167740226332631766)
XLA Ops:
  6.5 0.0 reduce-scatter.2.cloned.1.call-start
  6.5 8.6 %copy.11 = bf16[64,384,96]{2,0,1:T(8,128)(2,1)} copy(bf16[64,384,96]{1,2,0:T(8,128)(2,1)} %param.6) | data formatting | bytes 9437184 | tf_op args[0]
  15.2 82.1 %all_to_all.18 = bf16[64,384,96]{2,0,1:T(8,128)(2,1)S(1)} all-to-all(bf16[64,384,96]{2,0,1:T(8,128)(2,1)} %copy.11), channel_id=1, replica_groups=mesh['amp'=16,'int'=8] {'amp'}, dimensions={1} | all-to-all | bytes 9437184 | tf_op jit(solution)/shard_map/all_to_all | solution.py:19
  97.3 5.3 %copy.13 = bf16[16,64,24,96]{3,2,1,0:T(8,128)(2,1)S(1)} copy(bf16[16,64,24,96]{3,1,2,0:T(8,128)(2,1)S(1)} %bitcast.7) | data formatting | bytes 9437184 | tf_op jit(solution)/shard_map/all_to_all | solution.py:19
  102.6 13.5 %fusion.2 = f32[1024,1536]{1,0:T(8,128)} fusion(bf16[24,96,1536]{2,1,0:T(8,128)(2,1)} %param.7, bf16[1024,24,96]{2,1,0:T(8,128)(2,1)S(1)} %bitcast.8), kind=kOutput, calls=%fused_computation.2 | convolution fusion | flops 7247757312 | bytes 18087936 | tf_op jit(solution)/shard_map/dot_general | solution.py:20
  116.1 0.0 copy-start
  116.1 0.0 copy-start.1
  116.1 0.0 copy-start.2
  116.1 0.0 copy-start.3
  116.1 0.0 reduce-scatter.2.cloned.1.call-update
  116.2 87.2 %reduce-scatter.2.cloned.1.call-done = f32[64,1536]{1,0:T(8,128)} async-done(((f32[1024,1536]{1,0:T(8,128)}), f32[64,1536]{1,0:T(8,128)}) %reduce-scatter.2.cloned.1.call-update) | async-done | bytes 393232 | tf_op jit(solution)/shard_map/reduce_scatter | solution.py:23
  203.4 1.4 constant_dynamic-slice_fusion.6
  204.8 2.9 %collective-permute-start.6 = (f32[64,192]{1,0:T(8,128)S(1)}, f32[64,192]{1,0:T(8,128)S(1)}, u32[]{:S(2)}, u32[]{:S(2)}) collective-permute-start(f32[64,192]{1,0:T(8,128)S(1)} %get-tuple-element.6), channel_id=1, source_target_pairs={{0,7},{1,0},{2,1},{3,2},{4,3},{5,4},{6,5},{7,6},{8,15},{9,8},{10,9... | collective-permute-start | bytes 147464 | tf_op jit(solution)/shard_map/ppermute | solution.py:14
  207.6 0.7 collective-permute-start.5
  208.4 1.8 collective-permute-start.4
  210.2 0.6 collective-permute-start.3
  210.8 2.3 collective-permute-start.2
  213.1 0.0 collective-permute-done.6
  213.1 2.5 %collective-permute-start.1 = (f32[64,192]{1,0:T(8,128)S(1)}, f32[64,192]{1,0:T(8,128)S(1)}, u32[]{:S(2)}, u32[]{:S(2)}) collective-permute-start(f32[64,192]{1,0:T(8,128)S(1)} %get-tuple-element.11), channel_id=1, source_target_pairs={{0,2},{1,3},{2,4},{3,5},{4,6},{5,7},{6,0},{7,1},{8,10},{9,11},{10,... | collective-permute-start | bytes 147464 | tf_op jit(solution)/shard_map/ppermute | solution.py:14
  215.5 0.0 collective-permute-done.5
  215.5 0.1 collective-permute-start
  215.6 0.0 collective-permute-done.4
  215.6 0.0 collective-permute-done.3
  215.6 0.8 collective-permute-done.2
  216.4 3.4 %collective-permute-done.1 = f32[64,192]{1,0:T(8,128)S(1)} collective-permute-done((f32[64,192]{1,0:T(8,128)S(1)}, f32[64,192]{1,0:T(8,128)S(1)}, u32[]{:S(2)}, u32[]{:S(2)}) %collective-permute-start.1) | collective-permute-done | bytes 49184 | tf_op jit(solution)/shard_map/ppermute | solution.py:14
  219.8 2.1 collective-permute-done
  221.9 0.0 copy-done
  221.9 0.0 copy-done.1
  221.9 0.0 copy-done.2
  221.9 0.0 copy-done.3
  221.9 1.6 divide_add_fusion
Async XLA Ops:
  6.5 196.9 %reduce-scatter.2.cloned.1.call-start = ((), (), s32[]{:S(2)}) async-start(), calls=%async_computation.2 | async-start | bytes 6684672 | tf_op jit(solution)/shard_map/reduce_scatter | solution.py:23
  116.1 105.8 %copy-start = (f32[64,192]{1,0:T(8,128)S(1)}, f32[64,192]{1,0:T(8,128)}, u32[]{:S(2)}) copy-start(f32[64,192]{1,0:T(8,128)} %param.8) | copy-start | bytes 147460
  116.1 105.8 %copy-start.1 = (f32[64,192]{1,0:T(8,128)S(1)}, f32[64,192]{1,0:T(8,128)}, u32[]{:S(2)}) copy-start(f32[64,192]{1,0:T(8,128)} %param.9) | copy-start | bytes 147460
  116.1 105.8 %copy-start.2 = (f32[192]{0:T(256)S(1)}, f32[192]{0:T(256)}, u32[]{:S(2)}) copy-start(f32[192]{0:T(256)} %param.11) | copy-start | bytes 2308
  116.1 105.8 %copy-start.3 = (f32[64]{0:T(128)S(1)}, f32[64]{0:T(128)}, u32[]{:S(2)}) copy-start(f32[64]{0:T(128)} %param.10) | copy-start | bytes 772
  204.8 8.3 %collective-permute-start.6 = (f32[64,192]{1,0:T(8,128)S(1)}, f32[64,192]{1,0:T(8,128)S(1)}, u32[]{:S(2)}, u32[]{:S(2)}) collective-permute-start(f32[64,192]{1,0:T(8,128)S(1)} %get-tuple-element.6), channel_id=1, source_target_pairs={{0,7},{1,0},{2,1},{3,2},{4,3},{5,4},{6,5},{7,6},{8,15},{9,8},{10,9... | collective-permute-start | bytes 147464 | tf_op jit(solution)/shard_map/ppermute | solution.py:14
  207.6 7.9 %collective-permute-start.5 = (f32[64,192]{1,0:T(8,128)S(1)}, f32[64,192]{1,0:T(8,128)S(1)}, u32[]{:S(2)}, u32[]{:S(2)}) collective-permute-start(f32[64,192]{1,0:T(8,128)S(1)} %get-tuple-element.7), channel_id=1, source_target_pairs={{0,6},{1,7},{2,0},{3,1},{4,2},{5,3},{6,4},{7,5},{8,14},{9,15},{10,... | collective-permute-start | bytes 147464 | tf_op jit(solution)/shard_map/ppermute | solution.py:14
  208.4 7.3 %collective-permute-start.4 = (f32[64,192]{1,0:T(8,128)S(1)}, f32[64,192]{1,0:T(8,128)S(1)}, u32[]{:S(2)}, u32[]{:S(2)}) collective-permute-start(f32[64,192]{1,0:T(8,128)S(1)} %get-tuple-element.8), channel_id=1, source_target_pairs={{0,5},{1,6},{2,7},{3,0},{4,1},{5,2},{6,3},{7,4},{8,13},{9,14},{10,... | collective-permute-start | bytes 147464 | tf_op jit(solution)/shard_map/ppermute | solution.py:14
  210.2 5.4 %collective-permute-start.3 = (f32[64,192]{1,0:T(8,128)S(1)}, f32[64,192]{1,0:T(8,128)S(1)}, u32[]{:S(2)}, u32[]{:S(2)}) collective-permute-start(f32[64,192]{1,0:T(8,128)S(1)} %get-tuple-element.9), channel_id=1, source_target_pairs={{0,4},{1,5},{2,6},{3,7},{4,0},{5,1},{6,2},{7,3},{8,12},{9,13},{10,... | collective-permute-start | bytes 147464 | tf_op jit(solution)/shard_map/ppermute | solution.py:14
  210.8 5.6 %collective-permute-start.2 = (f32[64,192]{1,0:T(8,128)S(1)}, f32[64,192]{1,0:T(8,128)S(1)}, u32[]{:S(2)}, u32[]{:S(2)}) collective-permute-start(f32[64,192]{1,0:T(8,128)S(1)} %get-tuple-element.10), channel_id=1, source_target_pairs={{0,3},{1,4},{2,5},{3,6},{4,7},{5,0},{6,1},{7,2},{8,11},{9,12},{10,... | collective-permute-start | bytes 147464 | tf_op jit(solution)/shard_map/ppermute | solution.py:14
  213.1 6.7 %collective-permute-start.1 = (f32[64,192]{1,0:T(8,128)S(1)}, f32[64,192]{1,0:T(8,128)S(1)}, u32[]{:S(2)}, u32[]{:S(2)}) collective-permute-start(f32[64,192]{1,0:T(8,128)S(1)} %get-tuple-element.11), channel_id=1, source_target_pairs={{0,2},{1,3},{2,4},{3,5},{4,6},{5,7},{6,0},{7,1},{8,10},{9,11},{10,... | collective-permute-start | bytes 147464 | tf_op jit(solution)/shard_map/ppermute | solution.py:14
  215.5 6.4 %collective-permute-start = (f32[64,192]{1,0:T(8,128)S(1)}, f32[64,192]{1,0:T(8,128)S(1)}, u32[]{:S(2)}, u32[]{:S(2)}) collective-permute-start(f32[64,192]{1,0:T(8,128)S(1)} %get-tuple-element.5), channel_id=1, source_target_pairs={{0,1},{1,2},{2,3},{3,4},{4,5},{5,6},{6,7},{7,0},{8,9},{9,10},{10,1... | collective-permute-start | bytes 147464 | tf_op jit(solution)/shard_map/ppermute | solution.py:14
Sparse Core Ops, SparseCore 0:
  116.3 87.1 reduce-scatter.1

commit v2 on v1

--- a/solution.py
+++ b/solution.py
@@ -15,12 +15,38 @@
     return total
 
 
+def stage_sum(x, me_digit, size, stride, n):
+    total = lax.dynamic_index_in_dim(x, me_digit, 0, keepdims=False)
+    for s in range(1, size):
+        block = lax.dynamic_index_in_dim(x, (me_digit + s) % size, 0, keepdims=False)
+        perm = []
+        for i in range(n):
+            d = (i // stride) % size
+            perm.append((i, i + (((d + s) % size) - d) * stride))
+        total = total + lax.ppermute(block, "amp", perm)
+    return total
+
+
+def amp_reduce(partial, n_hi, n_z, n_core):
+    n = n_hi * n_z * n_core
+    me = lax.axis_index("amp")
+    core = me % n_core
+    z = (me // n_core) % n_z
+    hi = me // (n_core * n_z)
+    rows = partial.shape[0] // n
+    x = partial.reshape(n_hi, n_z, n_core, rows, -1)
+    x = stage_sum(jnp.moveaxis(x, 2, 0), core, n_core, 1, n)
+    x = stage_sum(jnp.moveaxis(x, 1, 0), z, n_z, n_core, n)
+    x = stage_sum(x, hi, n_hi, n_core * n_z, n)
+    return x
+
+
 def local(amplitudes, integrals, rest_residual, old_amplitudes, pair_energy, virt_energy):
     regrouped = lax.all_to_all(amplitudes, "amp", split_axis=1, concat_axis=0, tiled=True)
     partial = lax.dot_general(
         regrouped, integrals, (((1, 2), (0, 1)), ((), ())), preferred_element_type=jnp.float32
     )
-    rows = lax.psum_scatter(partial, "amp", scatter_dimension=0, tiled=True)
+    rows = amp_reduce(partial, 2, 4, 2)
     ladder = scatter_sum(rows, "int", 1)
     denominator = pair_energy[:, None] - virt_energy[None, :]
     return 0.4 * old_amplitudes + 0.6 * (ladder + rest_residual) / denominator

time: 231 us -> 212 us (0.918)
  blocking collectives: 82.1 us -> 0 us
  waiting for transfers between devices: 93.5 us -> 144 us
  starting transfers between devices: 10.8 us -> 34.3 us
  between operations: 13.5 us -> 0.24 us
  other arithmetic: 1.64 us -> 7.17 us
  matrix products: 13.5 us -> 10.5 us
    reduce_scatter x1 -> x0, waiting for transfers between devices: 87.2 us -> none  [local(): rows = lax.psum_scatter(partial, 'amp', scatter_dimension=0, tiled=True)]
    all_to_all x0 -> x1, waiting for transfers between devices: none -> 86.8 us  [local(): lax.all_to_all(amplitudes, 'amp', split_axis=1, concat_axis=0, tiled=True)]
    all_to_all x1 -> x0, blocking collectives: 82.1 us -> none  [local(): lax.all_to_all(amplitudes, 'amp', split_axis=1, concat_axis=0, tiled=True)]
    ppermute x0 -> x5, waiting for transfers between devices: none -> 51.2 us  [stage_sum(): total = total + lax.ppermute(block, 'amp', perm)]
    ppermute x0 -> x5, starting transfers between devices: none -> 14.8 us  [stage_sum(): total = total + lax.ppermute(block, 'amp', perm)]
    all_to_all x0 -> x1, starting transfers between devices: none -> 8.01 us  [local(): lax.all_to_all(amplitudes, 'amp', split_axis=1, concat_axis=0, tiled=True)]
    add x0 -> x3, other arithmetic: none -> 6.43 us  [stage_sum(): total = total + lax.ppermute(block, 'amp', perm)]
    all_to_all x1 -> x0, local copies, waits for them, and re-layouts: 5.27 us -> none  [local(): lax.all_to_all(amplitudes, 'amp', split_axis=1, concat_axis=0, tiled=True)]
  transfers between devices with their start and end apart: 8 -> 13, of which waited for: 4 -> 9; matrix products, arithmetic and copies ran while one was open for 0% -> 0% of each run, Pallas kernels for 0% -> 0%
where the time goes in v2:
time: 212 us; the launch traced here: 211 us
  waiting for transfers between devices  144 us (68%)
  starting transfers between devices  34.3 us (16%)
  local copies, waits for them, and re-layouts  14.1 us (7%)
  matrix products  10.5 us (5%)
  other arithmetic  7.17 us (3%)
    all_to_all x1, waiting for transfers between devices, local(): lax.all_to_all(amplitudes, 'amp', split_axis=1, concat_axis=0, tiled=True)  86.8 us
    ppermute x5, waiting for transfers between devices, stage_sum(): total = total + lax.ppermute(block, 'amp', perm)  51.2 us
    ppermute x5, starting transfers between devices, stage_sum(): total = total + lax.ppermute(block, 'amp', perm)  14.8 us
    unnamed x13, local copies, waits for them, and re-layouts  12.2 us
    ppermute x7, starting transfers between devices, scatter_sum(): lax.ppermute(block, axis_name, [(i, (i + s) % n) for i in range(n)])  11.4 us
    dot_general x1, matrix products, local(): lax.dot_general(regrouped, integrals, (((1, 2), (0, 1)), ((), ())), prefe...  10.5 us
    all_to_all x1, starting transfers between devices, local(): lax.all_to_all(amplitudes, 'amp', split_axis=1, concat_axis=0, tiled=True)  8.01 us
    add x3, other arithmetic, stage_sum(): total = total + lax.ppermute(block, 'amp', perm)  6.43 us
  transfers between devices with their start and end apart: 13, of which 9 were waited for; matrix products, arithmetic and copies ran while one was open for 0% of the time, Pallas kernels for 0%

profile of v2, /device:TPU:0, one launch (start us, length us, event | category | flops | bytes accessed | tf_op | source)
XLA Modules:
  0.0 210.7 jit_solution(16499851888779527436)
XLA Ops:
  0.0 8.7 %copy.10 = bf16[64,384,96]{2,0,1:T(8,128)(2,1)} copy(bf16[64,384,96]{1,2,0:T(8,128)(2,1)} %param.6) | data formatting | bytes 9437184 | tf_op args[0]
  8.7 8.0 %all-to-all-start = ((bf16[64,384,96]{2,0,1:T(8,128)(2,1)}), bf16[64,384,96]{2,0,1:T(8,128)(2,1)}, u32[]{:S(2)}, u32[]{:S(2)}) async-start(bf16[64,384,96]{2,0,1:T(8,128)(2,1)} %copy.10), calls=%async_computation | async-start | bytes 12582912 | tf_op jit(solution)/shard_map/all_to_all | solution.py:45
  16.7 86.8 %all-to-all-done = bf16[64,384,96]{2,0,1:T(8,128)(2,1)} async-done(((bf16[64,384,96]{2,0,1:T(8,128)(2,1)}), bf16[64,384,96]{2,0,1:T(8,128)(2,1)}, u32[]{:S(2)}, u32[]{:S(2)}) %all-to-all-start) | async-done | bytes 4718624 | tf_op jit(solution)/shard_map/all_to_all | solution.py:45
  103.6 10.5 %fusion.2 = f32[2,4,2,64,1536]{4,3,2,1,0:T(8,128)S(1)} fusion(bf16[2,4,2,64,24,96]{5,3,4,2,1,0:T(8,128)(2,1)} %bitcast.3, bf16[24,96,1536]{2,1,0:T(8,128)(2,1)} %param.7), kind=kOutput, calls=%fused_computation.2 | convolution fusion | flops 7247757312 | bytes 18087936 | tf_op jit(solution)/shard_map/dot_general | solution.py:46
  114.1 0.0 copy-start
  114.1 2.7 %copy-done = f32[2,4,2,64,1536]{4,3,2,1,0:T(8,128)} copy-done((f32[2,4,2,64,1536]{4,3,2,1,0:T(8,128)}, f32[2,4,2,64,1536]{4,3,2,1,0:T(8,128)S(1)}, u32[]{:S(2)}) %copy-start) | copy-done | bytes 6291480
  116.7 0.2 dynamic-slice_bitcast_fusion
  116.9 0.1 collective-permute-start
  117.1 5.7 %collective-permute-done = f32[2,4,64,1536]{3,2,1,0:T(8,128)} collective-permute-done((f32[2,4,64,1536]{3,2,1,0:T(8,128)S(1)}, f32[2,4,64,1536]{3,2,1,0:T(8,128)}, u32[]{:S(2)}, u32[]{:S(2)}) %collective-permute-start) | collective-permute-done | bytes 3145760 | tf_op jit(solution)/shard_map/ppermute | solution.py:26
  122.8 3.6 %bitcast_add_fusion = f32[2,4,64,1536]{3,2,1,0:T(8,128)S(1)} fusion(f32[2,4,64,1536]{3,2,1,0:T(8,128)} %collective-permute-done, f32[2,4,2,64,1536]{4,3,2,1,0:T(8,128)} %copy-done, s32[]{:T(128)S(6)} %select_n.118), kind=kLoop, calls=%fused_computation.3 | loop fusion | flops 786432 | bytes 9437188 | tf_op jit(solution)/shard_map/add | solution.py:26
  126.4 0.0 copy-start.2
  126.4 0.0 copy-start.3
  126.4 0.0 copy-start.4
  126.4 0.0 copy-start.5
  126.4 1.5 dynamic-slice_bitcast_fusion.3
  127.9 8.0 %collective-permute-start.3 = (f32[2,64,1536]{2,1,0:T(8,128)}, f32[2,64,1536]{2,1,0:T(8,128)}, u32[]{:S(2)}, u32[]{:S(2)}) collective-permute-start(f32[2,64,1536]{2,1,0:T(8,128)} %get-tuple-element.6), channel_id=1, source_target_pairs={{0,48},{8,56},{16,0},{24,8},{32,16},{40,24},{48,32},{56,40},{64,11... | collective-permute-start | bytes 2359304 | tf_op jit(solution)/shard_map/ppermute | solution.py:26
  135.9 1.6 collective-permute-start.2
  137.5 0.0 collective-permute-start.1
  137.5 32.9 %collective-permute-done.3 = f32[2,64,1536]{2,1,0:T(8,128)} collective-permute-done((f32[2,64,1536]{2,1,0:T(8,128)}, f32[2,64,1536]{2,1,0:T(8,128)}, u32[]{:S(2)}, u32[]{:S(2)}) %collective-permute-start.3) | collective-permute-done | bytes 786464 | tf_op jit(solution)/shard_map/ppermute | solution.py:26
  170.4 0.0 collective-permute-done.2
  170.4 3.7 %collective-permute-done.1 = f32[2,64,1536]{2,1,0:T(8,128)} collective-permute-done((f32[2,64,1536]{2,1,0:T(8,128)}, f32[2,64,1536]{2,1,0:T(8,128)}, u32[]{:S(2)}, u32[]{:S(2)}) %collective-permute-start.1) | collective-permute-done | bytes 786464 | tf_op jit(solution)/shard_map/ppermute | solution.py:26
  174.1 1.8 fusion.6
  175.9 0.0 copy-start.1
  175.9 0.9 copy-done.1
  176.8 5.1 %collective-permute-start.4 = (f32[64,1536]{1,0:T(8,128)S(1)}, f32[64,1536]{1,0:T(8,128)S(1)}, u32[]{:S(2)}, u32[]{:S(2)}) collective-permute-start(f32[64,1536]{1,0:T(8,128)S(1)} %dynamic-slice_bitcast_fusion.4), channel_id=1, source_target_pairs={{0,64},{8,72},{16,80},{24,88},{32,96},{40,104},{48,112},{56,120},{... | collective-permute-start | bytes 1179656 | tf_op jit(solution)/shard_map/ppermute | solution.py:26
  181.9 9.0 %collective-permute-done.4 = f32[64,1536]{1,0:T(8,128)S(1)} collective-permute-done((f32[64,1536]{1,0:T(8,128)S(1)}, f32[64,1536]{1,0:T(8,128)S(1)}, u32[]{:S(2)}, u32[]{:S(2)}) %collective-permute-start.4) | collective-permute-done | bytes 393248 | tf_op jit(solution)/shard_map/ppermute | solution.py:26
  190.9 1.0 bitcast_add_fusion.2
  192.0 0.2 constant_dynamic-slice_fusion.6
  192.2 5.0 %collective-permute-start.11 = (f32[64,192]{1,0:T(8,128)S(1)}, f32[64,192]{1,0:T(8,128)S(1)}, u32[]{:S(2)}, u32[]{:S(2)}) collective-permute-start(f32[64,192]{1,0:T(8,128)S(1)} %get-tuple-element.9), channel_id=1, source_target_pairs={{0,7},{1,0},{2,1},{3,2},{4,3},{5,4},{6,5},{7,6},{8,15},{9,8},{10,9... | collective-permute-start | bytes 147464 | tf_op jit(solution)/shard_map/ppermute | solution.py:14
  197.1 0.6 collective-permute-start.10
  197.8 0.0 collective-permute-start.9
  197.8 2.4 %collective-permute-start.8 = (f32[64,192]{1,0:T(8,128)S(1)}, f32[64,192]{1,0:T(8,128)S(1)}, u32[]{:S(2)}, u32[]{:S(2)}) collective-permute-start(f32[64,192]{1,0:T(8,128)S(1)} %get-tuple-element.12), channel_id=1, source_target_pairs={{0,4},{1,5},{2,6},{3,7},{4,0},{5,1},{6,2},{7,3},{8,12},{9,13},{10,... | collective-permute-start | bytes 147464 | tf_op jit(solution)/shard_map/ppermute | solution.py:14
  200.2 0.8 collective-permute-start.7
  201.0 0.0 collective-permute-done.11
  201.0 2.6 %collective-permute-start.6 = (f32[64,192]{1,0:T(8,128)S(1)}, f32[64,192]{1,0:T(8,128)S(1)}, u32[]{:S(2)}, u32[]{:S(2)}) collective-permute-start(f32[64,192]{1,0:T(8,128)S(1)} %get-tuple-element.14), channel_id=1, source_target_pairs={{0,2},{1,3},{2,4},{3,5},{4,6},{5,7},{6,0},{7,1},{8,10},{9,11},{10,... | collective-permute-start | bytes 147464 | tf_op jit(solution)/shard_map/ppermute | solution.py:14
  203.6 0.0 collective-permute-done.10
  203.6 0.0 collective-permute-start.5
  203.6 0.2 collective-permute-done.9
  203.8 0.0 collective-permute-done.8
  203.8 1.6 collective-permute-done.7
  205.4 2.6 %collective-permute-done.6 = f32[64,192]{1,0:T(8,128)S(1)} collective-permute-done((f32[64,192]{1,0:T(8,128)S(1)}, f32[64,192]{1,0:T(8,128)S(1)}, u32[]{:S(2)}, u32[]{:S(2)}) %collective-permute-start.6) | collective-permute-done | bytes 49184 | tf_op jit(solution)/shard_map/ppermute | solution.py:14
  208.0 2.0 collective-permute-done.5
  210.0 0.0 copy-done.2
  210.0 0.0 copy-done.3
  210.0 0.0 copy-done.4
  210.0 0.0 copy-done.5
  210.0 0.7 divide_add_fusion
  (1 shorter events, 0.0 us)
Async XLA Ops:
  8.7 94.9 %all-to-all-start = ((bf16[64,384,96]{2,0,1:T(8,128)(2,1)}), bf16[64,384,96]{2,0,1:T(8,128)(2,1)}, u32[]{:S(2)}, u32[]{:S(2)}) async-start(bf16[64,384,96]{2,0,1:T(8,128)(2,1)} %copy.10), calls=%async_computation | async-start | bytes 12582912 | tf_op jit(solution)/shard_map/all_to_all | solution.py:45
  114.1 2.7 %copy-start = (f32[2,4,2,64,1536]{4,3,2,1,0:T(8,128)}, f32[2,4,2,64,1536]{4,3,2,1,0:T(8,128)S(1)}, u32[]{:S(2)}) copy-start(f32[2,4,2,64,1536]{4,3,2,1,0:T(8,128)S(1)} %fusion.2) | copy-start | bytes 18874372
  116.9 5.9 %collective-permute-start = (f32[2,4,64,1536]{3,2,1,0:T(8,128)S(1)}, f32[2,4,64,1536]{3,2,1,0:T(8,128)}, u32[]{:S(2)}, u32[]{:S(2)}) collective-permute-start(f32[2,4,64,1536]{3,2,1,0:T(8,128)S(1)} %dynamic-slice_bitcast_fusion), channel_id=1, source_target_pairs={{0,8},{8,0},{16,24},{24,16},{32,40},{40,32},{48,56},{56,48},{64,72... | collective-permute-start | bytes 9437192 | tf_op jit(solution)/shard_map/ppermute | solution.py:26
  126.4 83.6 %copy-start.2 = (f32[64,192]{1,0:T(8,128)S(1)}, f32[64,192]{1,0:T(8,128)}, u32[]{:S(2)}) copy-start(f32[64,192]{1,0:T(8,128)} %param.8) | copy-start | bytes 147460
  126.4 83.6 %copy-start.3 = (f32[64,192]{1,0:T(8,128)S(1)}, f32[64,192]{1,0:T(8,128)}, u32[]{:S(2)}) copy-start(f32[64,192]{1,0:T(8,128)} %param.9) | copy-start | bytes 147460
  126.4 83.6 %copy-start.4 = (f32[192]{0:T(256)S(1)}, f32[192]{0:T(256)}, u32[]{:S(2)}) copy-start(f32[192]{0:T(256)} %param.11) | copy-start | bytes 2308
  126.4 83.6 %copy-start.5 = (f32[64]{0:T(128)S(1)}, f32[64]{0:T(128)}, u32[]{:S(2)}) copy-start(f32[64]{0:T(128)} %param.10) | copy-start | bytes 772
  127.9 42.5 %collective-permute-start.3 = (f32[2,64,1536]{2,1,0:T(8,128)}, f32[2,64,1536]{2,1,0:T(8,128)}, u32[]{:S(2)}, u32[]{:S(2)}) collective-permute-start(f32[2,64,1536]{2,1,0:T(8,128)} %get-tuple-element.6), channel_id=1, source_target_pairs={{0,48},{8,56},{16,0},{24,8},{32,16},{40,24},{48,32},{56,40},{64,11... | collective-permute-start | bytes 2359304 | tf_op jit(solution)/shard_map/ppermute | solution.py:26
  135.9 34.5 %collective-permute-start.2 = (f32[2,64,1536]{2,1,0:T(8,128)}, f32[2,64,1536]{2,1,0:T(8,128)}, u32[]{:S(2)}, u32[]{:S(2)}) collective-permute-start(f32[2,64,1536]{2,1,0:T(8,128)} %get-tuple-element.7), channel_id=1, source_target_pairs={{0,32},{8,40},{16,48},{24,56},{32,0},{40,8},{48,16},{56,24},{64,96... | collective-permute-start | bytes 2359304 | tf_op jit(solution)/shard_map/ppermute | solution.py:26
  137.5 36.5 %collective-permute-start.1 = (f32[2,64,1536]{2,1,0:T(8,128)}, f32[2,64,1536]{2,1,0:T(8,128)}, u32[]{:S(2)}, u32[]{:S(2)}) collective-permute-start(f32[2,64,1536]{2,1,0:T(8,128)} %get-tuple-element.5), channel_id=1, source_target_pairs={{0,16},{8,24},{16,32},{24,40},{32,48},{40,56},{48,0},{56,8},{64,80... | collective-permute-start | bytes 2359304 | tf_op jit(solution)/shard_map/ppermute | solution.py:26
  175.9 0.9 copy-start.1
  176.8 14.1 %collective-permute-start.4 = (f32[64,1536]{1,0:T(8,128)S(1)}, f32[64,1536]{1,0:T(8,128)S(1)}, u32[]{:S(2)}, u32[]{:S(2)}) collective-permute-start(f32[64,1536]{1,0:T(8,128)S(1)} %dynamic-slice_bitcast_fusion.4), channel_id=1, source_target_pairs={{0,64},{8,72},{16,80},{24,88},{32,96},{40,104},{48,112},{56,120},{... | collective-permute-start | bytes 1179656 | tf_op jit(solution)/shard_map/ppermute | solution.py:26
  192.2 8.8 %collective-permute-start.11 = (f32[64,192]{1,0:T(8,128)S(1)}, f32[64,192]{1,0:T(8,128)S(1)}, u32[]{:S(2)}, u32[]{:S(2)}) collective-permute-start(f32[64,192]{1,0:T(8,128)S(1)} %get-tuple-element.9), channel_id=1, source_target_pairs={{0,7},{1,0},{2,1},{3,2},{4,3},{5,4},{6,5},{7,6},{8,15},{9,8},{10,9... | collective-permute-start | bytes 147464 | tf_op jit(solution)/shard_map/ppermute | solution.py:14
  197.1 6.5 %collective-permute-start.10 = (f32[64,192]{1,0:T(8,128)S(1)}, f32[64,192]{1,0:T(8,128)S(1)}, u32[]{:S(2)}, u32[]{:S(2)}) collective-permute-start(f32[64,192]{1,0:T(8,128)S(1)} %get-tuple-element.10), channel_id=1, source_target_pairs={{0,6},{1,7},{2,0},{3,1},{4,2},{5,3},{6,4},{7,5},{8,14},{9,15},{10,... | collective-permute-start | bytes 147464 | tf_op jit(solution)/shard_map/ppermute | solution.py:14
  197.8 6.0 %collective-permute-start.9 = (f32[64,192]{1,0:T(8,128)S(1)}, f32[64,192]{1,0:T(8,128)S(1)}, u32[]{:S(2)}, u32[]{:S(2)}) collective-permute-start(f32[64,192]{1,0:T(8,128)S(1)} %get-tuple-element.11), channel_id=1, source_target_pairs={{0,5},{1,6},{2,7},{3,0},{4,1},{5,2},{6,3},{7,4},{8,13},{9,14},{10,... | collective-permute-start | bytes 147464 | tf_op jit(solution)/shard_map/ppermute | solution.py:14
  197.8 6.0 %collective-permute-start.8 = (f32[64,192]{1,0:T(8,128)S(1)}, f32[64,192]{1,0:T(8,128)S(1)}, u32[]{:S(2)}, u32[]{:S(2)}) collective-permute-start(f32[64,192]{1,0:T(8,128)S(1)} %get-tuple-element.12), channel_id=1, source_target_pairs={{0,4},{1,5},{2,6},{3,7},{4,0},{5,1},{6,2},{7,3},{8,12},{9,13},{10,... | collective-permute-start | bytes 147464 | tf_op jit(solution)/shard_map/ppermute | solution.py:14
  200.2 5.2 %collective-permute-start.7 = (f32[64,192]{1,0:T(8,128)S(1)}, f32[64,192]{1,0:T(8,128)S(1)}, u32[]{:S(2)}, u32[]{:S(2)}) collective-permute-start(f32[64,192]{1,0:T(8,128)S(1)} %get-tuple-element.13), channel_id=1, source_target_pairs={{0,3},{1,4},{2,5},{3,6},{4,7},{5,0},{6,1},{7,2},{8,11},{9,12},{10,... | collective-permute-start | bytes 147464 | tf_op jit(solution)/shard_map/ppermute | solution.py:14
  201.0 7.0 %collective-permute-start.6 = (f32[64,192]{1,0:T(8,128)S(1)}, f32[64,192]{1,0:T(8,128)S(1)}, u32[]{:S(2)}, u32[]{:S(2)}) collective-permute-start(f32[64,192]{1,0:T(8,128)S(1)} %get-tuple-element.14), channel_id=1, source_target_pairs={{0,2},{1,3},{2,4},{3,5},{4,6},{5,7},{6,0},{7,1},{8,10},{9,11},{10,... | collective-permute-start | bytes 147464 | tf_op jit(solution)/shard_map/ppermute | solution.py:14
  203.6 6.4 %collective-permute-start.5 = (f32[64,192]{1,0:T(8,128)S(1)}, f32[64,192]{1,0:T(8,128)S(1)}, u32[]{:S(2)}, u32[]{:S(2)}) collective-permute-start(f32[64,192]{1,0:T(8,128)S(1)} %get-tuple-element.8), channel_id=1, source_target_pairs={{0,1},{1,2},{2,3},{3,4},{4,5},{5,6},{6,7},{7,0},{8,9},{9,10},{10,1... | collective-permute-start | bytes 147464 | tf_op jit(solution)/shard_map/ppermute | solution.py:14

commit v3 on v2

--- a/solution.py
+++ b/solution.py
@@ -2,6 +2,8 @@
 import jax.numpy as jnp
 from jax import lax
 from jax.sharding import PartitionSpec as P
+
+CHUNKS = 2
 
 
 def scatter_sum(x, axis_name, axis):
@@ -42,11 +44,17 @@
 
 
 def local(amplitudes, integrals, rest_residual, old_amplitudes, pair_energy, virt_energy):
-    regrouped = lax.all_to_all(amplitudes, "amp", split_axis=1, concat_axis=0, tiled=True)
-    partial = lax.dot_general(
-        regrouped, integrals, (((1, 2), (0, 1)), ((), ())), preferred_element_type=jnp.float32
-    )
-    rows = amp_reduce(partial, 2, 4, 2)
+    pairs = amplitudes.shape[0]
+    step = pairs // CHUNKS
+    pieces = []
+    for k in range(CHUNKS):
+        part = amplitudes[k * step:(k + 1) * step]
+        regrouped = lax.all_to_all(part, "amp", split_axis=1, concat_axis=0, tiled=True)
+        partial = lax.dot_general(
+            regrouped, integrals, (((1, 2), (0, 1)), ((), ())), preferred_element_type=jnp.float32
+        )
+        pieces.append(amp_reduce(partial, 2, 4, 2))
+    rows = jnp.concatenate(pieces, axis=0)
     ladder = scatter_sum(rows, "int", 1)
     denominator = pair_energy[:, None] - virt_energy[None, :]
     return 0.4 * old_amplitudes + 0.6 * (ladder + rest_residual) / denominator

time: 212 us -> 189 us (0.89)
  waiting for transfers between devices: 144 us -> 103 us
  starting transfers between devices: 34.3 us -> 49.9 us
  matrix products: 10.5 us -> 14.3 us
  other arithmetic: 7.17 us -> 5 us
    ppermute x5 -> x10, waiting for transfers between devices: 51.2 us -> 29.3 us  [stage_sum(): total = total + lax.ppermute(block, 'amp', perm)]
    all_to_all x1 -> x2, waiting for transfers between devices: 86.8 us -> 70.8 us  [local(): lax.all_to_all(part, 'amp', split_axis=1, concat_axis=0, tiled=True)]
    all_to_all x1 -> x2, starting transfers between devices: 8.01 us -> 17.9 us  [local(): lax.all_to_all(part, 'amp', split_axis=1, concat_axis=0, tiled=True)]
    slice x0 -> x1, local copies, waits for them, and re-layouts: none -> 4.3 us  [local(): part = amplitudes[k * step:(k + 1) * step]]
    ppermute x5 -> x10, starting transfers between devices: 14.8 us -> 19.1 us  [stage_sum(): total = total + lax.ppermute(block, 'amp', perm)]
    dot_general x1 -> x2, matrix products: 10.5 us -> 14.3 us  [local(): lax.dot_general(regrouped, integrals, (((1, 2), (0, 1)), ((), ())), prefe...]
    ppermute x7, waiting for transfers between devices: 6.38 us -> 2.61 us  [scatter_sum(): lax.ppermute(block, axis_name, [(i, (i + s) % n) for i in range(n)])]
    unnamed x13 -> x12, local copies, waits for them, and re-layouts: 12.2 us -> 8.49 us
  transfers between devices with their start and end apart: 13 -> 19, of which waited for: 9 -> 8; matrix products, arithmetic and copies ran while one was open for 0% -> 13% of each run, Pallas kernels for 0% -> 0%
where the time goes in v3:
time: 189 us; the launch traced here: 188 us
  waiting for transfers between devices  103 us (54%)
  starting transfers between devices  49.9 us (26%)
  local copies, waits for them, and re-layouts  15.8 us (8%)
  matrix products  14.3 us (8%)
  other arithmetic  5 us (3%)
    all_to_all x2, waiting for transfers between devices, local(): lax.all_to_all(part, 'amp', split_axis=1, concat_axis=0, tiled=True)  70.8 us
    ppermute x10, waiting for transfers between devices, stage_sum(): total = total + lax.ppermute(block, 'amp', perm)  29.3 us
    ppermute x10, starting transfers between devices, stage_sum(): total = total + lax.ppermute(block, 'amp', perm)  19.1 us
    all_to_all x2, starting transfers between devices, local(): lax.all_to_all(part, 'amp', split_axis=1, concat_axis=0, tiled=True)  17.9 us
    dot_general x2, matrix products, local(): lax.dot_general(regrouped, integrals, (((1, 2), (0, 1)), ((), ())), prefe...  14.3 us
    ppermute x7, starting transfers between devices, scatter_sum(): lax.ppermute(block, axis_name, [(i, (i + s) % n) for i in range(n)])  12.9 us
    unnamed x12, local copies, waits for them, and re-layouts  8.49 us
    slice x1, local copies, waits for them, and re-layouts, local(): part = amplitudes[k * step:(k + 1) * step]  4.3 us
  transfers between devices with their start and end apart: 19, of which 8 were waited for; matrix products, arithmetic and copies ran while one was open for 13% of the time, Pallas kernels for 0%

profile of v3, /device:TPU:0, one launch (start us, length us, event | category | flops | bytes accessed | tf_op | source)
XLA Modules:
  0.0 188.0 jit_solution(11925664269686027702)
XLA Ops:
  0.0 4.3 %fusion.32 = (bf16[32,384,96]{1,2,0:T(8,128)(2,1)}, bf16[32,384,96]{1,2,0:T(8,128)(2,1)S(1)}) fusion(bf16[64,384,96]{1,2,0:T(8,128)(2,1)} %param.6), kind=kLoop, calls=%fused_computation.61 | loop fusion | bytes 9437184 | tf_op jit(solution)/shard_map/slice | solution.py:51
  4.3 5.0 %copy.25 = bf16[32,384,96]{2,0,1:T(8,128)(2,1)} copy(bf16[32,384,96]{1,2,0:T(8,128)(2,1)} %get-tuple-element.5) | data formatting | bytes 4718592
  9.3 8.0 %all-to-all-start.1 = ((bf16[32,384,96]{2,0,1:T(8,128)(2,1)}), bf16[32,384,96]{2,0,1:T(8,128)(2,1)}, u32[]{:S(2)}, u32[]{:S(2)}) async-start(bf16[32,384,96]{2,0,1:T(8,128)(2,1)} %copy.25), calls=%async_computation.1 | async-start | bytes 6291456 | tf_op jit(solution)/shard_map/all_to_all | solution.py:52
  17.3 3.5 %copy.24 = bf16[32,384,96]{2,0,1:T(8,128)(2,1)} copy(bf16[32,384,96]{1,2,0:T(8,128)(2,1)S(1)} %get-tuple-element.6) | data formatting | bytes 4718592
  20.8 38.2 %all-to-all-done.1 = bf16[32,384,96]{2,0,1:T(8,128)(2,1)} async-done(((bf16[32,384,96]{2,0,1:T(8,128)(2,1)}), bf16[32,384,96]{2,0,1:T(8,128)(2,1)}, u32[]{:S(2)}, u32[]{:S(2)}) %all-to-all-start.1) | async-done | bytes 2359328 | tf_op jit(solution)/shard_map/all_to_all | solution.py:52
  59.0 9.9 %all-to-all-start = ((bf16[32,384,96]{2,0,1:T(8,128)(2,1)}), bf16[32,384,96]{2,0,1:T(8,128)(2,1)}, u32[]{:S(2)}, u32[]{:S(2)}) async-start(bf16[32,384,96]{2,0,1:T(8,128)(2,1)} %copy.24), calls=%async_computation | async-start | bytes 6291456 | tf_op jit(solution)/shard_map/all_to_all | solution.py:52
  68.9 7.2 %fusion.7 = f32[2,4,2,32,1536]{4,3,2,1,0:T(8,128)S(1)} fusion(bf16[2,4,2,32,24,96]{5,3,4,2,1,0:T(8,128)(2,1)} %bitcast.19, bf16[24,96,1536]{2,1,0:T(8,128)(2,1)} %param.7), kind=kOutput, calls=%fused_computation.5 | convolution fusion | flops 3623878656 | bytes 12582912 | tf_op jit(solution)/shard_map/dot_general | solution.py:53
  76.1 0.0 copy-start
  76.1 1.4 dynamic-slice_bitcast_fusion
  77.5 0.4 collective-permute-start.5
  77.9 32.7 %all-to-all-done = bf16[32,384,96]{2,0,1:T(8,128)(2,1)} async-done(((bf16[32,384,96]{2,0,1:T(8,128)(2,1)}), bf16[32,384,96]{2,0,1:T(8,128)(2,1)}, u32[]{:S(2)}, u32[]{:S(2)}) %all-to-all-start) | async-done | bytes 2359328 | tf_op jit(solution)/shard_map/all_to_all | solution.py:52
  110.6 0.0 copy-done
  110.6 7.2 %fusion.4 = f32[2,4,2,32,1536]{4,3,2,1,0:T(8,128)S(1)} fusion(bf16[2,4,2,32,24,96]{5,3,4,2,1,0:T(8,128)(2,1)} %bitcast.3, bf16[24,96,1536]{2,1,0:T(8,128)(2,1)} %param.7), kind=kOutput, calls=%fused_computation.4 | convolution fusion | flops 3623878656 | bytes 12582912 | tf_op jit(solution)/shard_map/dot_general | solution.py:53
  117.7 1.3 dynamic-slice_bitcast_fusion.1
  119.1 0.0 collective-permute-start
  119.1 0.0 collective-permute-done.5
  119.1 2.1 %bitcast_add_fusion = f32[2,4,32,1536]{3,2,1,0:T(8,128)S(1)} fusion(f32[2,4,32,1536]{3,2,1,0:T(8,128)} %collective-permute-done.5, f32[2,4,2,32,1536]{4,3,2,1,0:T(8,128)} %copy-done, s32[]{:T(128)S(6)} %select_n.142), kind=kLoop, calls=%fused_computation.6 | loop fusion | flops 393216 | bytes 4718596 | tf_op jit(solution)/shard_map/add | solution.py:28
  121.2 0.1 dynamic-slice_bitcast_fusion.4
  121.3 3.5 %collective-permute-start.6 = (f32[2,32,1536]{2,1,0:T(8,128)S(1)}, f32[2,32,1536]{2,1,0:T(8,128)S(1)}, u32[]{:S(2)}, u32[]{:S(2)}) collective-permute-start(f32[2,32,1536]{2,1,0:T(8,128)S(1)} %get-tuple-element.7), channel_id=1, source_target_pairs={{0,16},{8,24},{16,32},{24,40},{32,48},{40,56},{48,0},{56,8},{64,80... | collective-permute-start | bytes 1179656 | tf_op jit(solution)/shard_map/ppermute | solution.py:28
  124.7 3.9 %collective-permute-start.7 = (f32[2,32,1536]{2,1,0:T(8,128)S(1)}, f32[2,32,1536]{2,1,0:T(8,128)S(1)}, u32[]{:S(2)}, u32[]{:S(2)}) collective-permute-start(f32[2,32,1536]{2,1,0:T(8,128)S(1)} %get-tuple-element.9), channel_id=1, source_target_pairs={{0,32},{8,40},{16,48},{24,56},{32,0},{40,8},{48,16},{56,24},{64,96... | collective-permute-start | bytes 1179656 | tf_op jit(solution)/shard_map/ppermute | solution.py:28
  128.7 0.0 collective-permute-start.8
  128.7 0.0 collective-permute-done
  128.7 1.6 bitcast_add_fusion.1
  130.3 0.1 dynamic-slice_bitcast_fusion.7
  130.4 2.1 %collective-permute-start.1 = (f32[2,32,1536]{2,1,0:T(8,128)S(1)}, f32[2,32,1536]{2,1,0:T(8,128)S(1)}, u32[]{:S(2)}, u32[]{:S(2)}) collective-permute-start(f32[2,32,1536]{2,1,0:T(8,128)S(1)} %get-tuple-element.10), channel_id=1, source_target_pairs={{0,16},{8,24},{16,32},{24,40},{32,48},{40,56},{48,0},{56,8},{64,80... | collective-permute-start | bytes 1179656 | tf_op jit(solution)/shard_map/ppermute | solution.py:28
  132.5 0.0 collective-permute-start.2
  132.5 4.6 %collective-permute-done.6 = f32[2,32,1536]{2,1,0:T(8,128)S(1)} collective-permute-done((f32[2,32,1536]{2,1,0:T(8,128)S(1)}, f32[2,32,1536]{2,1,0:T(8,128)S(1)}, u32[]{:S(2)}, u32[]{:S(2)}) %collective-permute-start.6) | collective-permute-done | bytes 393248 | tf_op jit(solution)/shard_map/ppermute | solution.py:28
  137.1 0.0 copy-start.1
  137.1 0.0 copy-start.2
  137.1 0.0 copy-start.3
  137.1 0.0 copy-start.4
  137.1 2.1 %collective-permute-start.3 = (f32[2,32,1536]{2,1,0:T(8,128)S(1)}, f32[2,32,1536]{2,1,0:T(8,128)S(1)}, u32[]{:S(2)}, u32[]{:S(2)}) collective-permute-start(f32[2,32,1536]{2,1,0:T(8,128)S(1)} %get-tuple-element.11), channel_id=1, source_target_pairs={{0,48},{8,56},{16,0},{24,8},{32,16},{40,24},{48,32},{56,40},{64,11... | collective-permute-start | bytes 1179656 | tf_op jit(solution)/shard_map/ppermute | solution.py:28
  139.2 7.8 %collective-permute-done.7 = f32[2,32,1536]{2,1,0:T(8,128)S(1)} collective-permute-done((f32[2,32,1536]{2,1,0:T(8,128)S(1)}, f32[2,32,1536]{2,1,0:T(8,128)S(1)}, u32[]{:S(2)}, u32[]{:S(2)}) %collective-permute-start.7) | collective-permute-done | bytes 393248 | tf_op jit(solution)/shard_map/ppermute | solution.py:28
  147.1 0.0 collective-permute-done.8
  147.1 0.1 fusion.11
  147.2 3.6 %collective-permute-start.9 = (f32[32,1536]{1,0:T(8,128)S(1)}, f32[32,1536]{1,0:T(8,128)S(1)}, u32[]{:S(2)}, u32[]{:S(2)}) collective-permute-start(f32[32,1536]{1,0:T(8,128)S(1)} %dynamic-slice_bitcast_fusion.8), channel_id=1, source_target_pairs={{0,64},{8,72},{16,80},{24,88},{32,96},{40,104},{48,112},{56,120},{... | collective-permute-start | bytes 589832 | tf_op jit(solution)/shard_map/ppermute | solution.py:28
  150.8 2.8 %collective-permute-done.1 = f32[2,32,1536]{2,1,0:T(8,128)S(1)} collective-permute-done((f32[2,32,1536]{2,1,0:T(8,128)S(1)}, f32[2,32,1536]{2,1,0:T(8,128)S(1)}, u32[]{:S(2)}, u32[]{:S(2)}) %collective-permute-start.1) | collective-permute-done | bytes 393248 | tf_op jit(solution)/shard_map/ppermute | solution.py:28
  153.5 9.6 %collective-permute-done.2 = f32[2,32,1536]{2,1,0:T(8,128)S(1)} collective-permute-done((f32[2,32,1536]{2,1,0:T(8,128)S(1)}, f32[2,32,1536]{2,1,0:T(8,128)S(1)}, u32[]{:S(2)}, u32[]{:S(2)}) %collective-permute-start.2) | collective-permute-done | bytes 393248 | tf_op jit(solution)/shard_map/ppermute | solution.py:28
  163.2 0.0 collective-permute-done.3
  163.2 0.1 fusion.13
  163.3 3.6 %collective-permute-start.4 = (f32[32,1536]{1,0:T(8,128)S(1)}, f32[32,1536]{1,0:T(8,128)S(1)}, u32[]{:S(2)}, u32[]{:S(2)}) collective-permute-start(f32[32,1536]{1,0:T(8,128)S(1)} %dynamic-slice_bitcast_fusion.9), channel_id=1, source_target_pairs={{0,64},{8,72},{16,80},{24,88},{32,96},{40,104},{48,112},{56,120},{... | collective-permute-start | bytes 589832 | tf_op jit(solution)/shard_map/ppermute | solution.py:28
  166.9 0.0 collective-permute-done.9
  167.0 4.4 %collective-permute-done.4 = f32[32,1536]{1,0:T(8,128)S(1)} collective-permute-done((f32[32,1536]{1,0:T(8,128)S(1)}, f32[32,1536]{1,0:T(8,128)S(1)}, u32[]{:S(2)}, u32[]{:S(2)}) %collective-permute-start.4) | collective-permute-done | bytes 196640 | tf_op jit(solution)/shard_map/ppermute | solution.py:28
  171.4 0.2 fusion.26
  171.6 1.6 collective-permute-start.10
  173.3 2.9 %collective-permute-start.11 = (f32[64,192]{1,0:T(8,128)S(1)}, f32[64,192]{1,0:T(8,128)S(1)}, u32[]{:S(2)}, u32[]{:S(2)}) collective-permute-start(f32[64,192]{1,0:T(8,128)S(1)} %get-tuple-element.14), channel_id=1, source_target_pairs={{0,2},{1,3},{2,4},{3,5},{4,6},{5,7},{6,0},{7,1},{8,10},{9,11},{10,... | collective-permute-start | bytes 147464 | tf_op jit(solution)/shard_map/ppermute | solution.py:16
  176.2 2.9 %collective-permute-start.12 = (f32[64,192]{1,0:T(8,128)S(1)}, f32[64,192]{1,0:T(8,128)S(1)}, u32[]{:S(2)}, u32[]{:S(2)}) collective-permute-start(f32[64,192]{1,0:T(8,128)S(1)} %get-tuple-element.15), channel_id=1, source_target_pairs={{0,3},{1,4},{2,5},{3,6},{4,7},{5,0},{6,1},{7,2},{8,11},{9,12},{10,... | collective-permute-start | bytes 147464 | tf_op jit(solution)/shard_map/ppermute | solution.py:16
  179.1 0.0 collective-permute-start.13
  179.1 2.1 %collective-permute-start.14 = (f32[64,192]{1,0:T(8,128)S(1)}, f32[64,192]{1,0:T(8,128)S(1)}, u32[]{:S(2)}, u32[]{:S(2)}) collective-permute-start(f32[64,192]{1,0:T(8,128)S(1)} %get-tuple-element.17), channel_id=1, source_target_pairs={{0,5},{1,6},{2,7},{3,0},{4,1},{5,2},{6,3},{7,4},{8,13},{9,14},{10,... | collective-permute-start | bytes 147464 | tf_op jit(solution)/shard_map/ppermute | solution.py:16
  181.2 0.1 fusion.14
  181.3 0.0 collective-permute-done.10
  181.3 1.6 collective-permute-start.15
  182.9 0.0 collective-permute-done.11
  182.9 1.7 collective-permute-start.16
  184.6 0.0 collective-permute-done.12
  184.6 0.0 collective-permute-done.13
  184.6 0.0 collective-permute-done.14
  184.6 2.6 %collective-permute-done.15 = f32[64,192]{1,0:T(8,128)S(1)} collective-permute-done((f32[64,192]{1,0:T(8,128)S(1)}, f32[64,192]{1,0:T(8,128)S(1)}, u32[]{:S(2)}, u32[]{:S(2)}) %collective-permute-start.15) | collective-permute-done | bytes 49184 | tf_op jit(solution)/shard_map/ppermute | solution.py:16
  187.2 0.0 collective-permute-done.16
  187.2 0.0 copy-done.1
  187.2 0.0 copy-done.2
  187.2 0.0 copy-done.3
  187.2 0.0 copy-done.4
  187.2 0.8 multiply_add_fusion
  (4 shorter events, 0.1 us)
Async XLA Ops:
  9.3 49.7 %all-to-all-start.1 = ((bf16[32,384,96]{2,0,1:T(8,128)(2,1)}), bf16[32,384,96]{2,0,1:T(8,128)(2,1)}, u32[]{:S(2)}, u32[]{:S(2)}) async-start(bf16[32,384,96]{2,0,1:T(8,128)(2,1)} %copy.25), calls=%async_computation.1 | async-start | bytes 6291456 | tf_op jit(solution)/shard_map/all_to_all | solution.py:52
  59.0 51.6 %all-to-all-start = ((bf16[32,384,96]{2,0,1:T(8,128)(2,1)}), bf16[32,384,96]{2,0,1:T(8,128)(2,1)}, u32[]{:S(2)}, u32[]{:S(2)}) async-start(bf16[32,384,96]{2,0,1:T(8,128)(2,1)} %copy.24), calls=%async_computation | async-start | bytes 6291456 | tf_op jit(solution)/shard_map/all_to_all | solution.py:52
  76.1 34.5 %copy-start = (f32[2,4,2,32,1536]{4,3,2,1,0:T(8,128)}, f32[2,4,2,32,1536]{4,3,2,1,0:T(8,128)S(1)}, u32[]{:S(2)}) copy-start(f32[2,4,2,32,1536]{4,3,2,1,0:T(8,128)S(1)} %fusion.7) | copy-start | bytes 9437188
  77.5 41.5 %collective-permute-start.5 = (f32[2,4,32,1536]{3,2,1,0:T(8,128)}, f32[2,4,32,1536]{3,2,1,0:T(8,128)}, u32[]{:S(2)}, u32[]{:S(2)}) collective-permute-start(f32[2,4,32,1536]{3,2,1,0:T(8,128)} %dynamic-slice_bitcast_fusion), channel_id=1, source_target_pairs={{0,8},{8,0},{16,24},{24,16},{32,40},{40,32},{48,56},{56,48},{64,72... | collective-permute-start | bytes 4718600 | tf_op jit(solution)/shard_map/ppermute | solution.py:28
  119.1 9.6 %collective-permute-start = (f32[2,4,32,1536]{3,2,1,0:T(8,128)}, f32[2,4,32,1536]{3,2,1,0:T(8,128)}, u32[]{:S(2)}, u32[]{:S(2)}) collective-permute-start(f32[2,4,32,1536]{3,2,1,0:T(8,128)} %dynamic-slice_bitcast_fusion.1), channel_id=1, source_target_pairs={{0,8},{8,0},{16,24},{24,16},{32,40},{40,32},{48,56},{56,48},{64,72... | collective-permute-start | bytes 4718600 | tf_op jit(solution)/shard_map/ppermute | solution.py:28
  121.3 15.8 %collective-permute-start.6 = (f32[2,32,1536]{2,1,0:T(8,128)S(1)}, f32[2,32,1536]{2,1,0:T(8,128)S(1)}, u32[]{:S(2)}, u32[]{:S(2)}) collective-permute-start(f32[2,32,1536]{2,1,0:T(8,128)S(1)} %get-tuple-element.7), channel_id=1, source_target_pairs={{0,16},{8,24},{16,32},{24,40},{32,48},{40,56},{48,0},{56,8},{64,80... | collective-permute-start | bytes 1179656 | tf_op jit(solution)/shard_map/ppermute | solution.py:28
  124.7 22.3 %collective-permute-start.7 = (f32[2,32,1536]{2,1,0:T(8,128)S(1)}, f32[2,32,1536]{2,1,0:T(8,128)S(1)}, u32[]{:S(2)}, u32[]{:S(2)}) collective-permute-start(f32[2,32,1536]{2,1,0:T(8,128)S(1)} %get-tuple-element.9), channel_id=1, source_target_pairs={{0,32},{8,40},{16,48},{24,56},{32,0},{40,8},{48,16},{56,24},{64,96... | collective-permute-start | bytes 1179656 | tf_op jit(solution)/shard_map/ppermute | solution.py:28
  128.7 18.4 %collective-permute-start.8 = (f32[2,32,1536]{2,1,0:T(8,128)S(1)}, f32[2,32,1536]{2,1,0:T(8,128)S(1)}, u32[]{:S(2)}, u32[]{:S(2)}) collective-permute-start(f32[2,32,1536]{2,1,0:T(8,128)S(1)} %get-tuple-element.8), channel_id=1, source_target_pairs={{0,48},{8,56},{16,0},{24,8},{32,16},{40,24},{48,32},{56,40},{64,11... | collective-permute-start | bytes 1179656 | tf_op jit(solution)/shard_map/ppermute | solution.py:28
  130.4 23.1 %collective-permute-start.1 = (f32[2,32,1536]{2,1,0:T(8,128)S(1)}, f32[2,32,1536]{2,1,0:T(8,128)S(1)}, u32[]{:S(2)}, u32[]{:S(2)}) collective-permute-start(f32[2,32,1536]{2,1,0:T(8,128)S(1)} %get-tuple-element.10), channel_id=1, source_target_pairs={{0,16},{8,24},{16,32},{24,40},{32,48},{40,56},{48,0},{56,8},{64,80... | collective-permute-start | bytes 1179656 | tf_op jit(solution)/shard_map/ppermute | solution.py:28
  132.5 30.7 %collective-permute-start.2 = (f32[2,32,1536]{2,1,0:T(8,128)S(1)}, f32[2,32,1536]{2,1,0:T(8,128)S(1)}, u32[]{:S(2)}, u32[]{:S(2)}) collective-permute-start(f32[2,32,1536]{2,1,0:T(8,128)S(1)} %get-tuple-element.12), channel_id=1, source_target_pairs={{0,32},{8,40},{16,48},{24,56},{32,0},{40,8},{48,16},{56,24},{64,96... | collective-permute-start | bytes 1179656 | tf_op jit(solution)/shard_map/ppermute | solution.py:28
  137.1 50.1 %copy-start.1 = (f32[64,192]{1,0:T(8,128)S(1)}, f32[64,192]{1,0:T(8,128)}, u32[]{:S(2)}) copy-start(f32[64,192]{1,0:T(8,128)} %param.9) | copy-start | bytes 147460
  137.1 50.1 %copy-start.2 = (f32[64,192]{1,0:T(8,128)S(1)}, f32[64,192]{1,0:T(8,128)}, u32[]{:S(2)}) copy-start(f32[64,192]{1,0:T(8,128)} %param.8) | copy-start | bytes 147460
  137.1 50.1 %copy-start.3 = (f32[192]{0:T(256)S(1)}, f32[192]{0:T(256)}, u32[]{:S(2)}) copy-start(f32[192]{0:T(256)} %param.11) | copy-start | bytes 2308
  137.1 50.1 %copy-start.4 = (f32[64]{0:T(128)S(1)}, f32[64]{0:T(128)}, u32[]{:S(2)}) copy-start(f32[64]{0:T(128)} %param.10) | copy-start | bytes 772
  137.1 26.1 %collective-permute-start.3 = (f32[2,32,1536]{2,1,0:T(8,128)S(1)}, f32[2,32,1536]{2,1,0:T(8,128)S(1)}, u32[]{:S(2)}, u32[]{:S(2)}) collective-permute-start(f32[2,32,1536]{2,1,0:T(8,128)S(1)} %get-tuple-element.11), channel_id=1, source_target_pairs={{0,48},{8,56},{16,0},{24,8},{32,16},{40,24},{48,32},{56,40},{64,11... | collective-permute-start | bytes 1179656 | tf_op jit(solution)/shard_map/ppermute | solution.py:28
  147.2 19.7 %collective-permute-start.9 = (f32[32,1536]{1,0:T(8,128)S(1)}, f32[32,1536]{1,0:T(8,128)S(1)}, u32[]{:S(2)}, u32[]{:S(2)}) collective-permute-start(f32[32,1536]{1,0:T(8,128)S(1)} %dynamic-slice_bitcast_fusion.8), channel_id=1, source_target_pairs={{0,64},{8,72},{16,80},{24,88},{32,96},{40,104},{48,112},{56,120},{... | collective-permute-start | bytes 589832 | tf_op jit(solution)/shard_map/ppermute | solution.py:28
  163.3 8.0 %collective-permute-start.4 = (f32[32,1536]{1,0:T(8,128)S(1)}, f32[32,1536]{1,0:T(8,128)S(1)}, u32[]{:S(2)}, u32[]{:S(2)}) collective-permute-start(f32[32,1536]{1,0:T(8,128)S(1)} %dynamic-slice_bitcast_fusion.9), channel_id=1, source_target_pairs={{0,64},{8,72},{16,80},{24,88},{32,96},{40,104},{48,112},{56,120},{... | collective-permute-start | bytes 589832 | tf_op jit(solution)/shard_map/ppermute | solution.py:28
  171.6 9.7 %collective-permute-start.10 = (f32[64,192]{1,0:T(8,128)S(1)}, f32[64,192]{1,0:T(8,128)S(1)}, u32[]{:S(2)}, u32[]{:S(2)}) collective-permute-start(f32[64,192]{1,0:T(8,128)S(1)} %get-tuple-element.13), channel_id=1, source_target_pairs={{0,1},{1,2},{2,3},{3,4},{4,5},{5,6},{6,7},{7,0},{8,9},{9,10},{10,1... | collective-permute-start | bytes 147464 | tf_op jit(solution)/shard_map/ppermute | solution.py:16
  173.3 9.7 %collective-permute-start.11 = (f32[64,192]{1,0:T(8,128)S(1)}, f32[64,192]{1,0:T(8,128)S(1)}, u32[]{:S(2)}, u32[]{:S(2)}) collective-permute-start(f32[64,192]{1,0:T(8,128)S(1)} %get-tuple-element.14), channel_id=1, source_target_pairs={{0,2},{1,3},{2,4},{3,5},{4,6},{5,7},{6,0},{7,1},{8,10},{9,11},{10,... | collective-permute-start | bytes 147464 | tf_op jit(solution)/shard_map/ppermute | solution.py:16
  176.2 8.4 %collective-permute-start.12 = (f32[64,192]{1,0:T(8,128)S(1)}, f32[64,192]{1,0:T(8,128)S(1)}, u32[]{:S(2)}, u32[]{:S(2)}) collective-permute-start(f32[64,192]{1,0:T(8,128)S(1)} %get-tuple-element.15), channel_id=1, source_target_pairs={{0,3},{1,4},{2,5},{3,6},{4,7},{5,0},{6,1},{7,2},{8,11},{9,12},{10,... | collective-permute-start | bytes 147464 | tf_op jit(solution)/shard_map/ppermute | solution.py:16
  179.1 5.5 %collective-permute-start.13 = (f32[64,192]{1,0:T(8,128)S(1)}, f32[64,192]{1,0:T(8,128)S(1)}, u32[]{:S(2)}, u32[]{:S(2)}) collective-permute-start(f32[64,192]{1,0:T(8,128)S(1)} %get-tuple-element.16), channel_id=1, source_target_pairs={{0,4},{1,5},{2,6},{3,7},{4,0},{5,1},{6,2},{7,3},{8,12},{9,13},{10,... | collective-permute-start | bytes 147464 | tf_op jit(solution)/shard_map/ppermute | solution.py:16
  179.1 5.5 %collective-permute-start.14 = (f32[64,192]{1,0:T(8,128)S(1)}, f32[64,192]{1,0:T(8,128)S(1)}, u32[]{:S(2)}, u32[]{:S(2)}) collective-permute-start(f32[64,192]{1,0:T(8,128)S(1)} %get-tuple-element.17), channel_id=1, source_target_pairs={{0,5},{1,6},{2,7},{3,0},{4,1},{5,2},{6,3},{7,4},{8,13},{9,14},{10,... | collective-permute-start | bytes 147464 | tf_op jit(solution)/shard_map/ppermute | solution.py:16
  181.3 5.8 %collective-permute-start.15 = (f32[64,192]{1,0:T(8,128)S(1)}, f32[64,192]{1,0:T(8,128)S(1)}, u32[]{:S(2)}, u32[]{:S(2)}) collective-permute-start(f32[64,192]{1,0:T(8,128)S(1)} %get-tuple-element.18), channel_id=1, source_target_pairs={{0,6},{1,7},{2,0},{3,1},{4,2},{5,3},{6,4},{7,5},{8,14},{9,15},{10,... | collective-permute-start | bytes 147464 | tf_op jit(solution)/shard_map/ppermute | solution.py:16
  182.9 4.3 %collective-permute-start.16 = (f32[64,192]{1,0:T(8,128)S(1)}, f32[64,192]{1,0:T(8,128)S(1)}, u32[]{:S(2)}, u32[]{:S(2)}) collective-permute-start(f32[64,192]{1,0:T(8,128)S(1)} %fusion.14), channel_id=1, source_target_pairs={{0,7},{1,0},{2,1},{3,2},{4,3},{5,4},{6,5},{7,6},{8,15},{9,8},{10,9... | collective-permute-start | bytes 147464 | tf_op jit(solution)/shard_map/ppermute | solution.py:16

commit v4 on v3

--- a/solution.py
+++ b/solution.py
@@ -3,7 +3,7 @@
 from jax import lax
 from jax.sharding import PartitionSpec as P
 
-CHUNKS = 2
+CHUNKS = 3
 
 
 def scatter_sum(x, axis_name, axis):
@@ -45,10 +45,10 @@
 
 def local(amplitudes, integrals, rest_residual, old_amplitudes, pair_energy, virt_energy):
     pairs = amplitudes.shape[0]
-    step = pairs // CHUNKS
+    sizes = (24, 24, 16)
     pieces = []
     for k in range(CHUNKS):
-        part = amplitudes[k * step:(k + 1) * step]
+        part = amplitudes[sum(sizes[:k]):sum(sizes[:k + 1])]
         regrouped = lax.all_to_all(part, "amp", split_axis=1, concat_axis=0, tiled=True)
         partial = lax.dot_general(
             regrouped, integrals, (((1, 2), (0, 1)), ((), ())), preferred_element_type=jnp.float32

time: 189 us -> 185 us (0.979)
  waiting for transfers between devices: 103 us -> 92 us
  matrix products: 14.3 us -> 17.4 us
  starting transfers between devices: 49.9 us -> 52.6 us
    all_to_all x2 -> x3, waiting for transfers between devices: 70.8 us -> 57.9 us  [local(): lax.all_to_all(part, 'amp', split_axis=1, concat_axis=0, tiled=True)]
    dot_general x2 -> x3, matrix products: 14.3 us -> 17.4 us  [local(): lax.dot_general(regrouped, integrals, (((1, 2), (0, 1)), ((), ())), prefe...]
    ppermute x10 -> x15, waiting for transfers between devices: 29.3 us -> 31.3 us  [stage_sum(): total = total + lax.ppermute(block, 'amp', perm)]
    all_to_all x2 -> x3, starting transfers between devices: 17.9 us -> 19.6 us  [local(): lax.all_to_all(part, 'amp', split_axis=1, concat_axis=0, tiled=True)]
    unnamed x12 -> x17, local copies, waits for them, and re-layouts: 8.49 us -> 9.65 us
    ppermute x10 -> x15, starting transfers between devices: 19.1 us -> 20.2 us  [stage_sum(): total = total + lax.ppermute(block, 'amp', perm)]
    slice x1 -> x3, local copies, waits for them, and re-layouts: 4.3 us -> 3.64 us  [local(): part = amplitudes[sum(sizes[:k]):sum(sizes[:k + 1])]]
    add x6 -> x9, other arithmetic: 3.94 us -> 4.04 us  [stage_sum(): total = total + lax.ppermute(block, 'amp', perm)]
  transfers between devices with their start and end apart: 19 -> 25, of which waited for: 8 -> 13; matrix products, arithmetic and copies ran while one was open for 13% -> 18% of each run, Pallas kernels for 0% -> 0%
where the time goes in v4:
time: 185 us; the launch traced here: 184 us
  waiting for transfers between devices  92 us (50%)
  starting transfers between devices  52.6 us (28%)
  matrix products  17.4 us (9%)
  local copies, waits for them, and re-layouts  16.8 us (9%)
  other arithmetic  4.81 us (3%)
    all_to_all x3, waiting for transfers between devices, local(): lax.all_to_all(part, 'amp', split_axis=1, concat_axis=0, tiled=True)  57.9 us
    ppermute x15, waiting for transfers between devices, stage_sum(): total = total + lax.ppermute(block, 'amp', perm)  31.3 us
    ppermute x15, starting transfers between devices, stage_sum(): total = total + lax.ppermute(block, 'amp', perm)  20.2 us
    all_to_all x3, starting transfers between devices, local(): lax.all_to_all(part, 'amp', split_axis=1, concat_axis=0, tiled=True)  19.6 us
    dot_general x3, matrix products, local(): lax.dot_general(regrouped, integrals, (((1, 2), (0, 1)), ((), ())), prefe...  17.4 us
    ppermute x7, starting transfers between devices, scatter_sum(): lax.ppermute(block, axis_name, [(i, (i + s) % n) for i in range(n)])  12.7 us
    unnamed x17, local copies, waits for them, and re-layouts  9.65 us
    add x9, other arithmetic, stage_sum(): total = total + lax.ppermute(block, 'amp', perm)  4.04 us
  transfers between devices with their start and end apart: 25, of which 13 were waited for; matrix products, arithmetic and copies ran while one was open for 18% of the time, Pallas kernels for 0%

profile of v4, /device:TPU:0, one launch (start us, length us, event | category | flops | bytes accessed | tf_op | source)
XLA Modules:
  0.0 184.0 jit_solution(12865406380182153236)
XLA Ops:
  0.0 1.3 slice-done
  1.3 2.0 %copy.34 = bf16[16,384,96]{2,0,1:T(8,128)(2,1)} copy(bf16[16,384,96]{1,2,0:T(8,128)(2,1)S(1)} %slice-done) | data formatting | bytes 2359296
  3.3 8.0 %all-to-all-start.2 = ((bf16[16,384,96]{2,0,1:T(8,128)(2,1)}), bf16[16,384,96]{2,0,1:T(8,128)(2,1)}, u32[]{:S(2)}, u32[]{:S(2)}) async-start(bf16[16,384,96]{2,0,1:T(8,128)(2,1)} %copy.34), calls=%async_computation.2 | async-start | bytes 3145728 | tf_op jit(solution)/shard_map/all_to_all | solution.py:52
  11.5 2.4 %fusion.21 = (bf16[24,384,96]{1,2,0:T(8,128)(2,1)S(1)}, bf16[24,384,96]{1,2,0:T(8,128)(2,1)S(1)}) fusion(bf16[64,384,96]{1,2,0:T(8,128)(2,1)} %param.6), kind=kLoop, calls=%fused_computation.48 | loop fusion | bytes 7077888 | tf_op jit(solution)/shard_map/slice | solution.py:51
  13.9 2.7 %copy.32 = bf16[24,384,96]{2,0,1:T(8,128)(2,1)} copy(bf16[24,384,96]{1,2,0:T(8,128)(2,1)S(1)} %get-tuple-element.5) | data formatting | bytes 3538944
  16.6 2.7 %copy.33 = bf16[24,384,96]{2,0,1:T(8,128)(2,1)} copy(bf16[24,384,96]{1,2,0:T(8,128)(2,1)S(1)} %get-tuple-element.6) | data formatting | bytes 3538944
  19.3 15.7 %all-to-all-done.2 = bf16[16,384,96]{2,0,1:T(8,128)(2,1)} async-done(((bf16[16,384,96]{2,0,1:T(8,128)(2,1)}), bf16[16,384,96]{2,0,1:T(8,128)(2,1)}, u32[]{:S(2)}, u32[]{:S(2)}) %all-to-all-start.2) | async-done | bytes 1179680 | tf_op jit(solution)/shard_map/all_to_all | solution.py:52
  35.1 4.4 %all-to-all-start = ((bf16[24,384,96]{2,0,1:T(8,128)(2,1)}), bf16[24,384,96]{2,0,1:T(8,128)(2,1)S(1)}, u32[]{:S(2)}, u32[]{:S(2)}) async-start(bf16[24,384,96]{2,0,1:T(8,128)(2,1)} %copy.32), calls=%async_computation | async-start | bytes 4718592 | tf_op jit(solution)/shard_map/all_to_all | solution.py:52
  39.5 4.9 %fusion.12 = f32[2,4,2,16,1536]{4,3,2,1,0:T(8,128)S(1)} fusion(bf16[2,4,2,16,24,96]{5,3,4,2,1,0:T(8,128)(2,1)} %bitcast.34, bf16[24,96,1536]{2,1,0:T(8,128)(2,1)} %param.7), kind=kOutput, calls=%fused_computation.8 | convolution fusion | flops 1811939328 | bytes 9830400 | tf_op jit(solution)/shard_map/dot_general | solution.py:53
  44.4 1.0 dynamic-slice_bitcast_fusion.2
  45.4 0.4 copy-done.1
  45.8 0.4 collective-permute-start.10
  46.2 25.7 %all-to-all-done = bf16[24,384,96]{2,0,1:T(8,128)(2,1)S(1)} async-done(((bf16[24,384,96]{2,0,1:T(8,128)(2,1)}), bf16[24,384,96]{2,0,1:T(8,128)(2,1)S(1)}, u32[]{:S(2)}, u32[]{:S(2)}) %all-to-all-start) | async-done | bytes 1769504 | tf_op jit(solution)/shard_map/all_to_all | solution.py:52
  71.9 1.4 copy-done
  73.4 7.2 %all-to-all-start.1 = ((bf16[24,384,96]{2,0,1:T(8,128)(2,1)}), bf16[24,384,96]{2,0,1:T(8,128)(2,1)}, u32[]{:S(2)}, u32[]{:S(2)}) async-start(bf16[24,384,96]{2,0,1:T(8,128)(2,1)} %copy.33), calls=%async_computation.1 | async-start | bytes 4718592 | tf_op jit(solution)/shard_map/all_to_all | solution.py:52
  80.6 6.2 %fusion.6 = f32[2,4,2,24,1536]{4,3,2,1,0:T(8,128)S(1)} fusion(bf16[2,4,2,24,24,96]{5,3,4,2,1,0:T(8,128)(2,1)} %bitcast.102, bf16[24,96,1536]{2,1,0:T(8,128)(2,1)} %param.7), kind=kOutput, calls=%fused_computation.6 | convolution fusion | flops 2717908992 | bytes 11206656 | tf_op jit(solution)/shard_map/dot_general | solution.py:53
  86.9 1.2 dynamic-slice_bitcast_fusion.1
  88.0 0.4 collective-permute-start
  88.4 0.3 copy-done.2
  88.7 1.2 bitcast_add_fusion.2
  89.9 0.8 dynamic-slice_bitcast_fusion.11
  90.7 1.9 %collective-permute-start.11 = (f32[2,16,1536]{2,1,0:T(8,128)}, f32[2,16,1536]{2,1,0:T(8,128)S(1)}, u32[]{:S(2)}, u32[]{:S(2)}) collective-permute-start(f32[2,16,1536]{2,1,0:T(8,128)} %get-tuple-element.13), channel_id=1, source_target_pairs={{0,16},{8,24},{16,32},{24,40},{32,48},{40,56},{48,0},{56,8},{64,80... | collective-permute-start | bytes 589832 | tf_op jit(solution)/shard_map/ppermute | solution.py:28
  92.6 2.7 %collective-permute-start.12 = (f32[2,16,1536]{2,1,0:T(8,128)}, f32[2,16,1536]{2,1,0:T(8,128)}, u32[]{:S(2)}, u32[]{:S(2)}) collective-permute-start(f32[2,16,1536]{2,1,0:T(8,128)} %get-tuple-element.15), channel_id=1, source_target_pairs={{0,32},{8,40},{16,48},{24,56},{32,0},{40,8},{48,16},{56,24},{64,96... | collective-permute-start | bytes 589832 | tf_op jit(solution)/shard_map/ppermute | solution.py:28
  95.3 1.5 collective-permute-start.13
  96.7 16.5 %all-to-all-done.1 = bf16[24,384,96]{2,0,1:T(8,128)(2,1)} async-done(((bf16[24,384,96]{2,0,1:T(8,128)(2,1)}), bf16[24,384,96]{2,0,1:T(8,128)(2,1)}, u32[]{:S(2)}, u32[]{:S(2)}) %all-to-all-start.1) | async-done | bytes 1769504 | tf_op jit(solution)/shard_map/all_to_all | solution.py:52
  113.2 6.2 %fusion.9 = f32[2,4,2,24,1536]{4,3,2,1,0:T(8,128)S(1)} fusion(bf16[2,4,2,24,24,96]{5,3,4,2,1,0:T(8,128)(2,1)} %bitcast.19, bf16[24,96,1536]{2,1,0:T(8,128)(2,1)} %param.7), kind=kOutput, calls=%fused_computation.7 | convolution fusion | flops 2717908992 | bytes 11206656 | tf_op jit(solution)/shard_map/dot_general | solution.py:53
  119.5 3.2 %collective-permute-done.13 = f32[2,16,1536]{2,1,0:T(8,128)} collective-permute-done((f32[2,16,1536]{2,1,0:T(8,128)S(1)}, f32[2,16,1536]{2,1,0:T(8,128)}, u32[]{:S(2)}, u32[]{:S(2)}) %collective-permute-start.13) | collective-permute-done | bytes 196640 | tf_op jit(solution)/shard_map/ppermute | solution.py:28
  122.6 1.1 fusion.20
  123.7 2.2 %collective-permute-start.14 = (f32[16,1536]{1,0:T(8,128)S(1)}, f32[16,1536]{1,0:T(8,128)S(1)}, u32[]{:S(2)}, u32[]{:S(2)}) collective-permute-start(f32[16,1536]{1,0:T(8,128)S(1)} %dynamic-slice_bitcast_fusion.14), channel_id=1, source_target_pairs={{0,64},{8,72},{16,80},{24,88},{32,96},{40,104},{48,112},{56,120},{... | collective-permute-start | bytes 294920 | tf_op jit(solution)/shard_map/ppermute | solution.py:28
  125.9 0.1 dynamic-slice_bitcast_fusion
  126.0 0.1 collective-permute-start.5
  126.1 3.8 %collective-permute-done.14 = f32[16,1536]{1,0:T(8,128)S(1)} collective-permute-done((f32[16,1536]{1,0:T(8,128)S(1)}, f32[16,1536]{1,0:T(8,128)S(1)}, u32[]{:S(2)}, u32[]{:S(2)}) %collective-permute-start.14) | collective-permute-done | bytes 98336 | tf_op jit(solution)/shard_map/ppermute | solution.py:28
  130.0 1.4 bitcast_add_fusion.1
  131.4 0.1 dynamic-slice_bitcast_fusion.8
  131.4 0.1 collective-permute-start.1
  131.5 3.6 %collective-permute-start.2 = (f32[2,24,1536]{2,1,0:T(8,128)S(1)}, f32[2,24,1536]{2,1,0:T(8,128)S(1)}, u32[]{:S(2)}, u32[]{:S(2)}) collective-permute-start(f32[2,24,1536]{2,1,0:T(8,128)S(1)} %get-tuple-element.9), channel_id=1, source_target_pairs={{0,32},{8,40},{16,48},{24,56},{32,0},{40,8},{48,16},{56,24},{64,96... | collective-permute-start | bytes 884744 | tf_op jit(solution)/shard_map/ppermute | solution.py:28
  135.2 0.2 bitcast_add_fusion
  135.3 0.1 dynamic-slice_bitcast_fusion.5
  135.4 2.1 %collective-permute-start.6 = (f32[2,24,1536]{2,1,0:T(8,128)S(1)}, f32[2,24,1536]{2,1,0:T(8,128)S(1)}, u32[]{:S(2)}, u32[]{:S(2)}) collective-permute-start(f32[2,24,1536]{2,1,0:T(8,128)S(1)} %get-tuple-element.10), channel_id=1, source_target_pairs={{0,16},{8,24},{16,32},{24,40},{32,48},{40,56},{48,0},{56,8},{64,80... | collective-permute-start | bytes 884744 | tf_op jit(solution)/shard_map/ppermute | solution.py:28
  137.5 0.6 collective-permute-start.7
  138.1 10.0 %collective-permute-done.1 = f32[2,24,1536]{2,1,0:T(8,128)S(1)} collective-permute-done((f32[2,24,1536]{2,1,0:T(8,128)S(1)}, f32[2,24,1536]{2,1,0:T(8,128)S(1)}, u32[]{:S(2)}, u32[]{:S(2)}) %collective-permute-start.1) | collective-permute-done | bytes 294944 | tf_op jit(solution)/shard_map/ppermute | solution.py:28
  148.1 1.4 collective-permute-done.2
  149.5 0.4 collective-permute-done.3
  149.9 0.1 fusion.18
  150.0 2.5 %collective-permute-start.4 = (f32[24,1536]{1,0:T(8,128)S(1)}, f32[24,1536]{1,0:T(8,128)S(1)}, u32[]{:S(2)}, u32[]{:S(2)}) collective-permute-start(f32[24,1536]{1,0:T(8,128)S(1)} %dynamic-slice_bitcast_fusion.13), channel_id=1, source_target_pairs={{0,64},{8,72},{16,80},{24,88},{32,96},{40,104},{48,112},{56,120},{... | collective-permute-start | bytes 442376 | tf_op jit(solution)/shard_map/ppermute | solution.py:28
  152.5 0.9 collective-permute-done.6
  153.3 7.2 %collective-permute-done.7 = f32[2,24,1536]{2,1,0:T(8,128)S(1)} collective-permute-done((f32[2,24,1536]{2,1,0:T(8,128)S(1)}, f32[2,24,1536]{2,1,0:T(8,128)S(1)}, u32[]{:S(2)}, u32[]{:S(2)}) %collective-permute-start.7) | collective-permute-done | bytes 294944 | tf_op jit(solution)/shard_map/ppermute | solution.py:28
  160.6 0.1 fusion.16
  160.6 0.0 copy-start.3
  160.6 0.0 copy-start.4
  160.7 0.0 copy-start.5
  160.7 0.0 copy-start.6
  160.7 2.3 %collective-permute-start.9 = (f32[24,1536]{1,0:T(8,128)S(1)}, f32[24,1536]{1,0:T(8,128)S(1)}, u32[]{:S(2)}, u32[]{:S(2)}) collective-permute-start(f32[24,1536]{1,0:T(8,128)S(1)} %dynamic-slice_bitcast_fusion.12), channel_id=1, source_target_pairs={{0,64},{8,72},{16,80},{24,88},{32,96},{40,104},{48,112},{56,120},{... | collective-permute-start | bytes 442376 | tf_op jit(solution)/shard_map/ppermute | solution.py:28
  163.0 4.4 %collective-permute-done.9 = f32[24,1536]{1,0:T(8,128)S(1)} collective-permute-done((f32[24,1536]{1,0:T(8,128)S(1)}, f32[24,1536]{1,0:T(8,128)S(1)}, u32[]{:S(2)}, u32[]{:S(2)}) %collective-permute-start.9) | collective-permute-done | bytes 147488 | tf_op jit(solution)/shard_map/ppermute | solution.py:28
  167.5 0.2 constant_dynamic-slice_fusion.6
  167.7 1.6 collective-permute-start.15
  169.4 2.9 %collective-permute-start.16 = (f32[64,192]{1,0:T(8,128)S(1)}, f32[64,192]{1,0:T(8,128)S(1)}, u32[]{:S(2)}, u32[]{:S(2)}) collective-permute-start(f32[64,192]{1,0:T(8,128)S(1)} %get-tuple-element.22), channel_id=1, source_target_pairs={{0,2},{1,3},{2,4},{3,5},{4,6},{5,7},{6,0},{7,1},{8,10},{9,11},{10,... | collective-permute-start | bytes 147464 | tf_op jit(solution)/shard_map/ppermute | solution.py:16
  172.3 2.9 %collective-permute-start.17 = (f32[64,192]{1,0:T(8,128)S(1)}, f32[64,192]{1,0:T(8,128)S(1)}, u32[]{:S(2)}, u32[]{:S(2)}) collective-permute-start(f32[64,192]{1,0:T(8,128)S(1)} %get-tuple-element.21), channel_id=1, source_target_pairs={{0,3},{1,4},{2,5},{3,6},{4,7},{5,0},{6,1},{7,2},{8,11},{9,12},{10,... | collective-permute-start | bytes 147464 | tf_op jit(solution)/shard_map/ppermute | solution.py:16
  175.1 2.3 %collective-permute-start.19 = (f32[64,192]{1,0:T(8,128)S(1)}, f32[64,192]{1,0:T(8,128)S(1)}, u32[]{:S(2)}, u32[]{:S(2)}) collective-permute-start(f32[64,192]{1,0:T(8,128)S(1)} %get-tuple-element.19), channel_id=1, source_target_pairs={{0,5},{1,6},{2,7},{3,0},{4,1},{5,2},{6,3},{7,4},{8,13},{9,14},{10,... | collective-permute-start | bytes 147464 | tf_op jit(solution)/shard_map/ppermute | solution.py:16
  177.5 1.3 collective-permute-start.20
  178.8 1.7 collective-permute-start.21
  180.5 0.1 collective-permute-done.19
  180.6 2.6 %collective-permute-done.20 = f32[64,192]{1,0:T(8,128)S(1)} collective-permute-done((f32[64,192]{1,0:T(8,128)S(1)}, f32[64,192]{1,0:T(8,128)S(1)}, u32[]{:S(2)}, u32[]{:S(2)}) %collective-permute-start.20) | collective-permute-done | bytes 49184 | tf_op jit(solution)/shard_map/ppermute | solution.py:16
  183.3 0.7 divide_add_fusion
  (30 shorter events, 0.2 us)
Async XLA Ops:
  0.0 1.3 slice-start
  3.3 31.8 %all-to-all-start.2 = ((bf16[16,384,96]{2,0,1:T(8,128)(2,1)}), bf16[16,384,96]{2,0,1:T(8,128)(2,1)}, u32[]{:S(2)}, u32[]{:S(2)}) async-start(bf16[16,384,96]{2,0,1:T(8,128)(2,1)} %copy.34), calls=%async_computation.2 | async-start | bytes 3145728 | tf_op jit(solution)/shard_map/all_to_all | solution.py:52
  35.1 36.9 %all-to-all-start = ((bf16[24,384,96]{2,0,1:T(8,128)(2,1)}), bf16[24,384,96]{2,0,1:T(8,128)(2,1)S(1)}, u32[]{:S(2)}, u32[]{:S(2)}) async-start(bf16[24,384,96]{2,0,1:T(8,128)(2,1)} %copy.32), calls=%async_computation | async-start | bytes 4718592 | tf_op jit(solution)/shard_map/all_to_all | solution.py:52
  44.4 1.5 copy-start.1
  45.8 42.6 %collective-permute-start.10 = (f32[2,4,16,1536]{3,2,1,0:T(8,128)}, f32[2,4,16,1536]{3,2,1,0:T(8,128)}, u32[]{:S(2)}, u32[]{:S(2)}) collective-permute-start(f32[2,4,16,1536]{3,2,1,0:T(8,128)} %dynamic-slice_bitcast_fusion.2), channel_id=1, source_target_pairs={{0,8},{8,0},{16,24},{24,16},{32,40},{40,32},{48,56},{56,48},{64,72... | collective-permute-start | bytes 2359304 | tf_op jit(solution)/shard_map/ppermute | solution.py:28
  71.9 1.4 copy-start
  73.4 39.8 %all-to-all-start.1 = ((bf16[24,384,96]{2,0,1:T(8,128)(2,1)}), bf16[24,384,96]{2,0,1:T(8,128)(2,1)}, u32[]{:S(2)}, u32[]{:S(2)}) async-start(bf16[24,384,96]{2,0,1:T(8,128)(2,1)} %copy.33), calls=%async_computation.1 | async-start | bytes 4718592 | tf_op jit(solution)/shard_map/all_to_all | solution.py:52
  86.8 1.8 copy-start.2
  88.0 41.9 %collective-permute-start = (f32[2,4,24,1536]{3,2,1,0:T(8,128)}, f32[2,4,24,1536]{3,2,1,0:T(8,128)}, u32[]{:S(2)}, u32[]{:S(2)}) collective-permute-start(f32[2,4,24,1536]{3,2,1,0:T(8,128)} %dynamic-slice_bitcast_fusion.1), channel_id=1, source_target_pairs={{0,8},{8,0},{16,24},{24,16},{32,40},{40,32},{48,56},{56,48},{64,72... | collective-permute-start | bytes 3538952 | tf_op jit(solution)/shard_map/ppermute | solution.py:28
  90.7 28.7 %collective-permute-start.11 = (f32[2,16,1536]{2,1,0:T(8,128)}, f32[2,16,1536]{2,1,0:T(8,128)S(1)}, u32[]{:S(2)}, u32[]{:S(2)}) collective-permute-start(f32[2,16,1536]{2,1,0:T(8,128)} %get-tuple-element.13), channel_id=1, source_target_pairs={{0,16},{8,24},{16,32},{24,40},{32,48},{40,56},{48,0},{56,8},{64,80... | collective-permute-start | bytes 589832 | tf_op jit(solution)/shard_map/ppermute | solution.py:28
  92.6 26.9 %collective-permute-start.12 = (f32[2,16,1536]{2,1,0:T(8,128)}, f32[2,16,1536]{2,1,0:T(8,128)}, u32[]{:S(2)}, u32[]{:S(2)}) collective-permute-start(f32[2,16,1536]{2,1,0:T(8,128)} %get-tuple-element.15), channel_id=1, source_target_pairs={{0,32},{8,40},{16,48},{24,56},{32,0},{40,8},{48,16},{56,24},{64,96... | collective-permute-start | bytes 589832 | tf_op jit(solution)/shard_map/ppermute | solution.py:28
  95.3 27.4 %collective-permute-start.13 = (f32[2,16,1536]{2,1,0:T(8,128)S(1)}, f32[2,16,1536]{2,1,0:T(8,128)}, u32[]{:S(2)}, u32[]{:S(2)}) collective-permute-start(f32[2,16,1536]{2,1,0:T(8,128)S(1)} %get-tuple-element.14), channel_id=1, source_target_pairs={{0,48},{8,56},{16,0},{24,8},{32,16},{40,24},{48,32},{56,40},{64,11... | collective-permute-start | bytes 589832 | tf_op jit(solution)/shard_map/ppermute | solution.py:28
  123.7 6.2 %collective-permute-start.14 = (f32[16,1536]{1,0:T(8,128)S(1)}, f32[16,1536]{1,0:T(8,128)S(1)}, u32[]{:S(2)}, u32[]{:S(2)}) collective-permute-start(f32[16,1536]{1,0:T(8,128)S(1)} %dynamic-slice_bitcast_fusion.14), channel_id=1, source_target_pairs={{0,64},{8,72},{16,80},{24,88},{32,96},{40,104},{48,112},{56,120},{... | collective-permute-start | bytes 294920 | tf_op jit(solution)/shard_map/ppermute | solution.py:28
  126.0 9.2 %collective-permute-start.5 = (f32[2,4,24,1536]{3,2,1,0:T(8,128)S(1)}, f32[2,4,24,1536]{3,2,1,0:T(8,128)S(1)}, u32[]{:S(2)}, u32[]{:S(2)}) collective-permute-start(f32[2,4,24,1536]{3,2,1,0:T(8,128)S(1)} %dynamic-slice_bitcast_fusion), channel_id=1, source_target_pairs={{0,8},{8,0},{16,24},{24,16},{32,40},{40,32},{48,56},{56,48},{64,72... | collective-permute-start | bytes 3538952 | tf_op jit(solution)/shard_map/ppermute | solution.py:28
  131.4 16.6 %collective-permute-start.1 = (f32[2,24,1536]{2,1,0:T(8,128)S(1)}, f32[2,24,1536]{2,1,0:T(8,128)S(1)}, u32[]{:S(2)}, u32[]{:S(2)}) collective-permute-start(f32[2,24,1536]{2,1,0:T(8,128)S(1)} %get-tuple-element.7), channel_id=1, source_target_pairs={{0,16},{8,24},{16,32},{24,40},{32,48},{40,56},{48,0},{56,8},{64,80... | collective-permute-start | bytes 884744 | tf_op jit(solution)/shard_map/ppermute | solution.py:28
  131.5 17.9 %collective-permute-start.2 = (f32[2,24,1536]{2,1,0:T(8,128)S(1)}, f32[2,24,1536]{2,1,0:T(8,128)S(1)}, u32[]{:S(2)}, u32[]{:S(2)}) collective-permute-start(f32[2,24,1536]{2,1,0:T(8,128)S(1)} %get-tuple-element.9), channel_id=1, source_target_pairs={{0,32},{8,40},{16,48},{24,56},{32,0},{40,8},{48,16},{56,24},{64,96... | collective-permute-start | bytes 884744 | tf_op jit(solution)/shard_map/ppermute | solution.py:28
  135.2 14.7 %collective-permute-start.3 = (f32[2,24,1536]{2,1,0:T(8,128)S(1)}, f32[2,24,1536]{2,1,0:T(8,128)S(1)}, u32[]{:S(2)}, u32[]{:S(2)}) collective-permute-start(f32[2,24,1536]{2,1,0:T(8,128)S(1)} %get-tuple-element.8), channel_id=1, source_target_pairs={{0,48},{8,56},{16,0},{24,8},{32,16},{40,24},{48,32},{56,40},{64,11... | collective-permute-start | bytes 884744 | tf_op jit(solution)/shard_map/ppermute | solution.py:28
  135.4 17.9 %collective-permute-start.6 = (f32[2,24,1536]{2,1,0:T(8,128)S(1)}, f32[2,24,1536]{2,1,0:T(8,128)S(1)}, u32[]{:S(2)}, u32[]{:S(2)}) collective-permute-start(f32[2,24,1536]{2,1,0:T(8,128)S(1)} %get-tuple-element.10), channel_id=1, source_target_pairs={{0,16},{8,24},{16,32},{24,40},{32,48},{40,56},{48,0},{56,8},{64,80... | collective-permute-start | bytes 884744 | tf_op jit(solution)/shard_map/ppermute | solution.py:28
  137.5 23.0 %collective-permute-start.7 = (f32[2,24,1536]{2,1,0:T(8,128)S(1)}, f32[2,24,1536]{2,1,0:T(8,128)S(1)}, u32[]{:S(2)}, u32[]{:S(2)}) collective-permute-start(f32[2,24,1536]{2,1,0:T(8,128)S(1)} %get-tuple-element.12), channel_id=1, source_target_pairs={{0,32},{8,40},{16,48},{24,56},{32,0},{40,8},{48,16},{56,24},{64,96... | collective-permute-start | bytes 884744 | tf_op jit(solution)/shard_map/ppermute | solution.py:28
  148.1 12.5 %collective-permute-start.8 = (f32[2,24,1536]{2,1,0:T(8,128)S(1)}, f32[2,24,1536]{2,1,0:T(8,128)S(1)}, u32[]{:S(2)}, u32[]{:S(2)}) collective-permute-start(f32[2,24,1536]{2,1,0:T(8,128)S(1)} %get-tuple-element.11), channel_id=1, source_target_pairs={{0,48},{8,56},{16,0},{24,8},{32,16},{40,24},{48,32},{56,40},{64,11... | collective-permute-start | bytes 884744 | tf_op jit(solution)/shard_map/ppermute | solution.py:28
  150.0 13.0 %collective-permute-start.4 = (f32[24,1536]{1,0:T(8,128)S(1)}, f32[24,1536]{1,0:T(8,128)S(1)}, u32[]{:S(2)}, u32[]{:S(2)}) collective-permute-start(f32[24,1536]{1,0:T(8,128)S(1)} %dynamic-slice_bitcast_fusion.13), channel_id=1, source_target_pairs={{0,64},{8,72},{16,80},{24,88},{32,96},{40,104},{48,112},{56,120},{... | collective-permute-start | bytes 442376 | tf_op jit(solution)/shard_map/ppermute | solution.py:28
  160.6 22.6 %copy-start.3 = (f32[64,192]{1,0:T(8,128)S(1)}, f32[64,192]{1,0:T(8,128)}, u32[]{:S(2)}) copy-start(f32[64,192]{1,0:T(8,128)} %param.8) | copy-start | bytes 147460
  160.6 22.6 %copy-start.4 = (f32[64,192]{1,0:T(8,128)S(1)}, f32[64,192]{1,0:T(8,128)}, u32[]{:S(2)}) copy-start(f32[64,192]{1,0:T(8,128)} %param.9) | copy-start | bytes 147460
  160.7 22.6 %copy-start.5 = (f32[192]{0:T(256)S(1)}, f32[192]{0:T(256)}, u32[]{:S(2)}) copy-start(f32[192]{0:T(256)} %param.11) | copy-start | bytes 2308
  160.7 22.6 %copy-start.6 = (f32[64]{0:T(128)S(1)}, f32[64]{0:T(128)}, u32[]{:S(2)}) copy-start(f32[64]{0:T(128)} %param.10) | copy-start | bytes 772
  160.7 6.7 %collective-permute-start.9 = (f32[24,1536]{1,0:T(8,128)S(1)}, f32[24,1536]{1,0:T(8,128)S(1)}, u32[]{:S(2)}, u32[]{:S(2)}) collective-permute-start(f32[24,1536]{1,0:T(8,128)S(1)} %dynamic-slice_bitcast_fusion.12), channel_id=1, source_target_pairs={{0,64},{8,72},{16,80},{24,88},{32,96},{40,104},{48,112},{56,120},{... | collective-permute-start | bytes 442376 | tf_op jit(solution)/shard_map/ppermute | solution.py:28
  167.7 9.8 %collective-permute-start.15 = (f32[64,192]{1,0:T(8,128)S(1)}, f32[64,192]{1,0:T(8,128)S(1)}, u32[]{:S(2)}, u32[]{:S(2)}) collective-permute-start(f32[64,192]{1,0:T(8,128)S(1)} %get-tuple-element.16), channel_id=1, source_target_pairs={{0,1},{1,2},{2,3},{3,4},{4,5},{5,6},{6,7},{7,0},{8,9},{9,10},{10,1... | collective-permute-start | bytes 147464 | tf_op jit(solution)/shard_map/ppermute | solution.py:16
  169.4 9.4 %collective-permute-start.16 = (f32[64,192]{1,0:T(8,128)S(1)}, f32[64,192]{1,0:T(8,128)S(1)}, u32[]{:S(2)}, u32[]{:S(2)}) collective-permute-start(f32[64,192]{1,0:T(8,128)S(1)} %get-tuple-element.22), channel_id=1, source_target_pairs={{0,2},{1,3},{2,4},{3,5},{4,6},{5,7},{6,0},{7,1},{8,10},{9,11},{10,... | collective-permute-start | bytes 147464 | tf_op jit(solution)/shard_map/ppermute | solution.py:16
  172.3 8.2 %collective-permute-start.17 = (f32[64,192]{1,0:T(8,128)S(1)}, f32[64,192]{1,0:T(8,128)S(1)}, u32[]{:S(2)}, u32[]{:S(2)}) collective-permute-start(f32[64,192]{1,0:T(8,128)S(1)} %get-tuple-element.21), channel_id=1, source_target_pairs={{0,3},{1,4},{2,5},{3,6},{4,7},{5,0},{6,1},{7,2},{8,11},{9,12},{10,... | collective-permute-start | bytes 147464 | tf_op jit(solution)/shard_map/ppermute | solution.py:16
  175.1 5.3 %collective-permute-start.18 = (f32[64,192]{1,0:T(8,128)S(1)}, f32[64,192]{1,0:T(8,128)S(1)}, u32[]{:S(2)}, u32[]{:S(2)}) collective-permute-start(f32[64,192]{1,0:T(8,128)S(1)} %get-tuple-element.20), channel_id=1, source_target_pairs={{0,4},{1,5},{2,6},{3,7},{4,0},{5,1},{6,2},{7,3},{8,12},{9,13},{10,... | collective-permute-start | bytes 147464 | tf_op jit(solution)/shard_map/ppermute | solution.py:16
  175.1 5.5 %collective-permute-start.19 = (f32[64,192]{1,0:T(8,128)S(1)}, f32[64,192]{1,0:T(8,128)S(1)}, u32[]{:S(2)}, u32[]{:S(2)}) collective-permute-start(f32[64,192]{1,0:T(8,128)S(1)} %get-tuple-element.19), channel_id=1, source_target_pairs={{0,5},{1,6},{2,7},{3,0},{4,1},{5,2},{6,3},{7,4},{8,13},{9,14},{10,... | collective-permute-start | bytes 147464 | tf_op jit(solution)/shard_map/ppermute | solution.py:16
  177.5 5.8 %collective-permute-start.20 = (f32[64,192]{1,0:T(8,128)S(1)}, f32[64,192]{1,0:T(8,128)S(1)}, u32[]{:S(2)}, u32[]{:S(2)}) collective-permute-start(f32[64,192]{1,0:T(8,128)S(1)} %get-tuple-element.18), channel_id=1, source_target_pairs={{0,6},{1,7},{2,0},{3,1},{4,2},{5,3},{6,4},{7,5},{8,14},{9,15},{10,... | collective-permute-start | bytes 147464 | tf_op jit(solution)/shard_map/ppermute | solution.py:16
  178.8 4.4 %collective-permute-start.21 = (f32[64,192]{1,0:T(8,128)S(1)}, f32[64,192]{1,0:T(8,128)S(1)}, u32[]{:S(2)}, u32[]{:S(2)}) collective-permute-start(f32[64,192]{1,0:T(8,128)S(1)} %get-tuple-element.17), channel_id=1, source_target_pairs={{0,7},{1,0},{2,1},{3,2},{4,3},{5,4},{6,5},{7,6},{8,15},{9,8},{10,9... | collective-permute-start | bytes 147464 | tf_op jit(solution)/shard_map/ppermute | solution.py:16

commit v5 on v2

v5 whole, which is shorter than its diff:
```python
import jax
import jax.numpy as jnp
from jax import lax
from jax.sharding import PartitionSpec as P

SIZES = (24, 24, 16)


def stage_sum(x, me_digit, size, stride, n):
    total = lax.dynamic_index_in_dim(x, me_digit, 0, keepdims=False)
    for s in range(1, size):
        block = lax.dynamic_index_in_dim(x, (me_digit + s) % size, 0, keepdims=False)
        perm = []
        for i in range(n):
            d = (i // stride) % size
            perm.append((i, i + (((d + s) % size) - d) * stride))
        total = total + lax.ppermute(block, "amp", perm)
    return total


def local(amplitudes, integrals, rest_residual, old_amplitudes, pair_energy, virt_energy):
    n_hi, n_z, n_core = 2, 4, 2
    n = n_hi * n_z * n_core
    n_chips = n // n_core
    me = lax.axis_index("amp")
    core = me % n_core
    z = (me // n_core) % n_z
    hi = me // (n_core * n_z)
    pairs, cw, dl = amplitudes.shape
    width = cw // n
    sibling = lax.ppermute(integrals, "amp", [(i, i ^ 1) for i in range(n)])
    groups = [[c + n_core * m for m in range(n_chips)] for c in range(n_core)]
    dims = (((1, 2), (0, 1)), ((), ()))
    pieces = []
    start = 0
    for size in SIZES:
        part = amplitudes[start:start + size]
        start += size
        got = lax.all_to_all(
            part, "amp", split_axis=1, concat_axis=0, tiled=True, axis_index_groups=groups
        )
        own = lax.dynamic_slice_in_dim(got, core * width, width, axis=1)
        other = lax.dynamic_slice_in_dim(got, (1 - core) * width, width, axis=1)
        partial = lax.dot_general(own, integrals, dims, preferred_element_type=jnp.float32)
        partial = partial + lax.dot_general(other, sibling, dims, preferred_element_type=jnp.float32)
        x = partial.reshape(n_hi, n_z, size, -1)
        x = stage_sum(jnp.moveaxis(x, 1, 0), z, n_z, n_core, n)
        pieces.append(stage_sum(x, hi, n_hi, n_core * n_z, n))
    rows = jnp.concatenate(pieces, axis=0)
    n_int = lax.axis_size("int")
    blocks = rows.reshape(rows.shape[0], n_int, -1)
    ladder = lax.all_to_all(blocks, "int", split_axis=1, concat_axis=1, tiled=True).sum(axis=1)
    denominator = pair_energy[:, None] - virt_energy[None, :]
    return 0.4 * old_amplitudes + 0.6 * (ladder + rest_residual) / denominator


def solution(mesh):
    placed = (
        P("amp", None, "int"),
        P("amp", "int", None),
        P("amp", "int"),
        P("amp", "int"),
        P("amp"),
        P("int"),
    )
    return jax.shard_map(
        local, mesh=mesh, in_specs=placed, out_specs=P("amp", "int"), check_vma=False
    )
```

time: 212 us -> 176 us (0.83)
  waiting for transfers between devices: 144 us -> 81.9 us
  blocking collectives: 0 us -> 12.9 us
  matrix products: 10.5 us -> 23.2 us
  local copies, waits for them, and re-layouts: 14.1 us -> 21.2 us
  other arithmetic: 7.17 us -> 1.04 us
    ppermute x5 -> x12, waiting for transfers between devices: 51.2 us -> 21.9 us  [stage_sum(): total = total + lax.ppermute(block, 'amp', perm)]
    all_to_all x1 -> x3, waiting for transfers between devices: 86.8 us -> 60 us  [local(): lax.all_to_all(part, 'amp', split_axis=1, concat_axis=0, tiled=True, axis...]
    all_to_all x0 -> x1, blocking collectives: none -> 12.9 us  [local(): lax.all_to_all(blocks, 'int', split_axis=1, concat_axis=1, tiled=True)]
    dot_general x1 -> x6, matrix products: 10.5 us -> 23.2 us  [the longest x3 12.3 us: local(): lax.dot_general(other, sibling, dims, preferred_element_type=jnp.float32)]
    ppermute x7 -> x1, starting transfers between devices: 11.4 us -> 0.01 us  [local(): sibling = lax.ppermute(integrals, 'amp', [(i, i ^ 1) for i in range(n)])]
    all_to_all x1 -> x3, starting transfers between devices: 8.01 us -> 17.4 us  [local(): lax.all_to_all(part, 'amp', split_axis=1, concat_axis=0, tiled=True, axis...]
    all_to_all x0 -> x3, local copies, waits for them, and re-layouts: none -> 6.4 us  [local(): lax.all_to_all(part, 'amp', split_axis=1, concat_axis=0, tiled=True, axis...]
    ppermute x7 -> x1, waiting for transfers between devices: 6.38 us -> 0.01 us  [local(): sibling = lax.ppermute(integrals, 'amp', [(i, i ^ 1) for i in range(n)])]
  transfers between devices with their start and end apart: 13 -> 16, of which waited for: 9 -> 8; matrix products, arithmetic and copies ran while one was open for 0% -> 22% of each run, Pallas kernels for 0% -> 0%
where the time goes in v5:
time: 176 us
  waiting for transfers between devices  81.9 us (47%)
  starting transfers between devices  35.3 us (20%)
  matrix products  23.2 us (13%)
  local copies, waits for them, and re-layouts  21.2 us (12%)
  blocking collectives  12.9 us (7%)
    all_to_all x3, waiting for transfers between devices, local(): lax.all_to_all(part, 'amp', split_axis=1, concat_axis=0, tiled=True, axis...  60 us
    ppermute x12, waiting for transfers between devices, stage_sum(): total = total + lax.ppermute(block, 'amp', perm)  21.9 us
    ppermute x12, starting transfers between devices, stage_sum(): total = total + lax.ppermute(block, 'amp', perm)  17.9 us
    all_to_all x3, starting transfers between devices, local(): lax.all_to_all(part, 'amp', split_axis=1, concat_axis=0, tiled=True, axis...  17.4 us
    all_to_all x1, blocking collectives, local(): lax.all_to_all(blocks, 'int', split_axis=1, concat_axis=1, tiled=True)  12.9 us
    dot_general x3, matrix products, local(): lax.dot_general(other, sibling, dims, preferred_element_type=jnp.float32)  12.3 us
    dot_general x3, matrix products, local(): lax.dot_general(own, integrals, dims, preferred_element_type=jnp.float32)  10.9 us
    unnamed x19, local copies, waits for them, and re-layouts  9.05 us
  transfers between devices with their start and end apart: 16, of which 8 were waited for; matrix products, arithmetic and copies ran while one was open for 22% of the time, Pallas kernels for 0%

profile of v5, /device:TPU:0, one launch (start us, length us, event | category | flops | bytes accessed | tf_op | source)
XLA Modules:
  0.0 175.9 jit_solution(7621998041454629611)
XLA Ops:
  0.0 0.0 collective-permute-start
  0.0 1.3 slice-done
  1.3 2.1 %copy.46 = bf16[16,384,96]{2,0,1:T(8,128)(2,1)} copy(bf16[16,384,96]{1,2,0:T(8,128)(2,1)S(1)} %slice-done) | data formatting | bytes 2359296
  3.3 7.9 %all-to-all-start.2 = ((bf16[16,384,96]{2,0,1:T(8,128)(2,1)}), bf16[16,384,96]{2,0,1:T(8,128)(2,1)}, u32[]{:S(2)}, u32[]{:S(2)}) async-start(bf16[16,384,96]{2,0,1:T(8,128)(2,1)} %copy.46), calls=%async_computation.2 | async-start | bytes 3145728 | tf_op jit(solution)/shard_map/all_to_all | solution.py:39
  11.2 3.7 %fusion.19 = (bf16[24,384,96]{1,2,0:T(8,128)(2,1)S(1)}, bf16[24,384,96]{1,2,0:T(8,128)(2,1)}) fusion(bf16[64,384,96]{1,2,0:T(8,128)(2,1)} %param.6), kind=kLoop, calls=%fused_computation.47 | loop fusion | bytes 7077888 | tf_op jit(solution)/shard_map/slice | solution.py:37
  14.9 2.7 %copy.44 = bf16[24,384,96]{2,0,1:T(8,128)(2,1)} copy(bf16[24,384,96]{1,2,0:T(8,128)(2,1)S(1)} %get-tuple-element.5) | data formatting | bytes 3538944
  17.6 14.5 %all-to-all-done.2 = bf16[16,384,96]{2,0,1:T(8,128)(2,1)} async-done(((bf16[16,384,96]{2,0,1:T(8,128)(2,1)}), bf16[16,384,96]{2,0,1:T(8,128)(2,1)}, u32[]{:S(2)}, u32[]{:S(2)}) %all-to-all-start.2) | async-done | bytes 1179680 | tf_op jit(solution)/shard_map/all_to_all | solution.py:39
  32.1 4.8 %all-to-all-start = ((bf16[24,384,96]{2,0,1:T(8,128)(2,1)}), bf16[24,384,96]{2,0,1:T(8,128)(2,1)S(1)}, u32[]{:S(2)}, u32[]{:S(2)}) async-start(bf16[24,384,96]{2,0,1:T(8,128)(2,1)} %copy.44), calls=%async_computation | async-start | bytes 4718592 | tf_op jit(solution)/shard_map/all_to_all | solution.py:39
  36.8 4.2 %copy.45 = bf16[24,384,96]{2,0,1:T(8,128)(2,1)} copy(bf16[24,384,96]{1,2,0:T(8,128)(2,1)} %get-tuple-element.6) | data formatting | bytes 3538944
  41.0 25.2 %all-to-all-done = bf16[24,384,96]{2,0,1:T(8,128)(2,1)S(1)} async-done(((bf16[24,384,96]{2,0,1:T(8,128)(2,1)}), bf16[24,384,96]{2,0,1:T(8,128)(2,1)S(1)}, u32[]{:S(2)}, u32[]{:S(2)}) %all-to-all-start) | async-done | bytes 1769504 | tf_op jit(solution)/shard_map/all_to_all | solution.py:39
  66.2 4.8 %all-to-all-start.1 = ((bf16[24,384,96]{2,0,1:T(8,128)(2,1)}), bf16[24,384,96]{2,0,1:T(8,128)(2,1)}, u32[]{:S(2)}, u32[]{:S(2)}) async-start(bf16[24,384,96]{2,0,1:T(8,128)(2,1)} %copy.45), calls=%async_computation.1 | async-start | bytes 4718592 | tf_op jit(solution)/shard_map/all_to_all | solution.py:39
  71.0 1.8 %copy.37 = bf16[8,16,48,96]{3,2,1,0:T(8,128)(2,1)S(1)} copy(bf16[8,16,48,96]{3,1,2,0:T(8,128)(2,1)} %bitcast.28) | data formatting | bytes 2359296 | tf_op jit(solution)/shard_map/all_to_all | solution.py:39
  72.8 0.3 constant_dynamic-slice_fusion
  73.1 5.1 %convolution_bitcast_fusion.5 = f32[128,1536]{1,0:T(8,128)} fusion(bf16[24,96,1536]{2,1,0:T(8,128)(2,1)} %param.7, bf16[128,24,96]{2,1,0:T(8,128)(2,1)S(1)} %get-tuple-element.8), kind=kOutput, calls=%fused_computation.7 | convolution fusion | flops 905969664 | bytes 8454144 | tf_op jit(solution)/shard_map/dot_general | solution.py:44
  78.2 2.1 %copy.31 = bf16[8,24,48,96]{3,1,0,2:T(8,128)(2,1)} copy(bf16[8,24,48,96]{3,1,2,0:T(8,128)(2,1)S(1)} %bitcast.87) | data formatting | bytes 3538944 | tf_op jit(solution)/shard_map/all_to_all | solution.py:39
  80.3 20.2 %all-to-all-done.1 = bf16[24,384,96]{2,0,1:T(8,128)(2,1)} async-done(((bf16[24,384,96]{2,0,1:T(8,128)(2,1)}), bf16[24,384,96]{2,0,1:T(8,128)(2,1)}, u32[]{:S(2)}, u32[]{:S(2)}) %all-to-all-start.1) | async-done | bytes 1769504 | tf_op jit(solution)/shard_map/all_to_all | solution.py:39
  100.5 2.5 %copy.34 = bf16[8,24,48,96]{3,1,0,2:T(8,128)(2,1)S(1)} copy(bf16[8,24,48,96]{3,1,2,0:T(8,128)(2,1)} %bitcast.15) | data formatting | bytes 3538944 | tf_op jit(solution)/shard_map/all_to_all | solution.py:39
  103.0 0.0 copy-done
  103.0 0.0 slice-start.2
  103.0 4.2 %convolution_bitcast_fusion.3 = f32[192,1536]{1,0:T(8,128)S(1)} fusion(bf16[24,96,1536]{2,1,0:T(8,128)(2,1)} %param.7, bf16[192,48,96]{2,0,1:T(8,128)(2,1)S(1)} %bitcast.91, s32[]{:T(128)S(6)} %select_n.95), kind=kOutput, calls=%fused_computation.3 | convolution fusion | flops 1358954496 | bytes 9437188 | tf_op jit(solution)/shard_map/dot_general | solution.py:44
  107.2 0.0 slice-done.1
  107.2 0.1 slice-done.2
  107.3 1.6 convolution_bitcast_fusion.1
  108.9 0.0 collective-permute-done
  108.9 4.1 %fusion = f32[192,1536]{1,0:T(8,128)S(1)} fusion(f32[192,1536]{1,0:T(8,128)S(1)} %convolution_bitcast_fusion.3, bf16[24,96,1536]{2,1,0:T(8,128)(2,1)} %collective-permute-done, bf16[192,48,96]{2,0,1:T(8,128)(2,1)S(1)} %bitcast.92, s32[]{:T(128)S(6)} %select_n.96), kind=kOutput, calls=%fused_computation.4 | convolution fusion | flops 1359249408 | bytes 10616836 | tf_op jit(solution)/shard_map/dot_general | solution.py:45
  113.1 0.1 dynamic-slice_bitcast_fusion.5
  113.1 1.6 collective-permute-start.1
  114.7 3.0 %collective-permute-start.2 = (f32[2,24,1536]{2,1,0:T(8,128)S(1)}, f32[2,24,1536]{2,1,0:T(8,128)S(1)}, u32[]{:S(2)}, u32[]{:S(2)}) collective-permute-start(f32[2,24,1536]{2,1,0:T(8,128)S(1)} %get-tuple-element.11), channel_id=1, source_target_pairs={{0,32},{8,40},{16,48},{24,56},{32,0},{40,8},{48,16},{56,24},{64,96... | collective-permute-start | bytes 884744 | tf_op jit(solution)/shard_map/ppermute | solution.py:17
  117.7 4.2 %fusion.2 = f32[128,1536]{1,0:T(8,128)S(1)} fusion(f32[128,1536]{1,0:T(8,128)S(1)} %copy-done.5, bf16[24,96,1536]{2,1,0:T(8,128)(2,1)} %collective-permute-done, bf16[128,24,96]{2,1,0:T(8,128)(2,1)S(1)} %get-tuple-element.7), kind=kOutput, calls=%fused_computation.8 | convolution fusion | flops 906166272 | bytes 9240576 | tf_op jit(solution)/shard_map/dot_general | solution.py:45
  121.9 0.1 dynamic-slice_bitcast_fusion.8
  122.0 0.6 collective-permute-start.10
  122.6 1.7 collective-permute-start.11
  124.3 0.3 collective-permute-start.9
  124.6 4.0 %fusion.1 = f32[192,1536]{1,0:T(8,128)S(1)} fusion(f32[192,1536]{1,0:T(8,128)S(1)} %convolution_bitcast_fusion.1, bf16[24,96,1536]{2,1,0:T(8,128)(2,1)} %collective-permute-done, bf16[192,48,96]{2,0,1:T(8,128)(2,1)S(1)} %bitcast.90, s32[]{:T(128)S(6)} %select_n.96), kind=kOutput, calls=%fused_computation.5 | convolution fusion | flops 1359249408 | bytes 10616836 | tf_op jit(solution)/shard_map/dot_general | solution.py:45
  128.7 0.1 dynamic-slice_bitcast_fusion.2
  128.7 7.4 %collective-permute-done.10 = f32[2,16,1536]{2,1,0:T(8,128)S(1)} collective-permute-done((f32[2,16,1536]{2,1,0:T(8,128)S(1)}, f32[2,16,1536]{2,1,0:T(8,128)S(1)}, u32[]{:S(2)}, u32[]{:S(2)}) %collective-permute-start.10) | collective-permute-done | bytes 196640 | tf_op jit(solution)/shard_map/ppermute | solution.py:17
  136.2 0.0 collective-permute-start.3
  136.2 0.0 collective-permute-done.11
  136.2 2.0 %collective-permute-start.5 = (f32[2,24,1536]{2,1,0:T(8,128)S(1)}, f32[2,24,1536]{2,1,0:T(8,128)S(1)}, u32[]{:S(2)}, u32[]{:S(2)}) collective-permute-start(f32[2,24,1536]{2,1,0:T(8,128)S(1)} %get-tuple-element.12), channel_id=1, source_target_pairs={{0,16},{8,24},{16,32},{24,40},{32,48},{40,56},{48,0},{56,8},{64,80... | collective-permute-start | bytes 884744 | tf_op jit(solution)/shard_map/ppermute | solution.py:17
  138.2 0.0 collective-permute-done.9
  138.2 1.7 collective-permute-start.6
  140.0 0.0 collective-permute-done.1
  140.0 1.1 collective-permute-start.7
  141.1 0.0 collective-permute-done.2
  141.1 2.7 %collective-permute-start.12 = (f32[16,1536]{1,0:T(8,128)S(1)}, f32[16,1536]{1,0:T(8,128)S(1)}, u32[]{:S(2)}, u32[]{:S(2)}) collective-permute-start(f32[16,1536]{1,0:T(8,128)S(1)} %dynamic-slice_bitcast_fusion.11), channel_id=1, source_target_pairs={{0,64},{8,72},{16,80},{24,88},{32,96},{40,104},{48,112},{56,120},{... | collective-permute-start | bytes 294920 | tf_op jit(solution)/shard_map/ppermute | solution.py:17
  143.8 2.2 %collective-permute-done.3 = f32[2,24,1536]{2,1,0:T(8,128)S(1)} collective-permute-done((f32[2,24,1536]{2,1,0:T(8,128)S(1)}, f32[2,24,1536]{2,1,0:T(8,128)S(1)}, u32[]{:S(2)}, u32[]{:S(2)}) %collective-permute-start.3) | collective-permute-done | bytes 294944 | tf_op jit(solution)/shard_map/ppermute | solution.py:17
  146.0 0.1 fusion.12
  146.1 1.1 collective-permute-start.4
  147.2 0.0 collective-permute-done.5
  147.2 3.6 %collective-permute-done.6 = f32[2,24,1536]{2,1,0:T(8,128)S(1)} collective-permute-done((f32[2,24,1536]{2,1,0:T(8,128)S(1)}, f32[2,24,1536]{2,1,0:T(8,128)S(1)}, u32[]{:S(2)}, u32[]{:S(2)}) %collective-permute-start.6) | collective-permute-done | bytes 294944 | tf_op jit(solution)/shard_map/ppermute | solution.py:17
  150.8 4.1 %collective-permute-done.7 = f32[2,24,1536]{2,1,0:T(8,128)S(1)} collective-permute-done((f32[2,24,1536]{2,1,0:T(8,128)S(1)}, f32[2,24,1536]{2,1,0:T(8,128)S(1)}, u32[]{:S(2)}, u32[]{:S(2)}) %collective-permute-start.7) | collective-permute-done | bytes 294944 | tf_op jit(solution)/shard_map/ppermute | solution.py:17
  154.9 0.1 fusion.10
  155.0 2.1 %collective-permute-start.8 = (f32[24,1536]{1,0:T(8,128)S(1)}, f32[24,1536]{1,0:T(8,128)S(1)}, u32[]{:S(2)}, u32[]{:S(2)}) collective-permute-start(f32[24,1536]{1,0:T(8,128)S(1)} %dynamic-slice_bitcast_fusion.9), channel_id=1, source_target_pairs={{0,64},{8,72},{16,80},{24,88},{32,96},{40,104},{48,112},{56,120},{... | collective-permute-start | bytes 442376 | tf_op jit(solution)/shard_map/ppermute | solution.py:17
  157.1 0.0 collective-permute-done.12
  157.1 0.0 collective-permute-done.4
  157.2 0.0 copy-start.1
  157.2 0.0 copy-start.2
  157.2 0.0 copy-start.3
  157.2 0.0 copy-start.4
  157.2 4.5 %collective-permute-done.8 = f32[24,1536]{1,0:T(8,128)S(1)} collective-permute-done((f32[24,1536]{1,0:T(8,128)S(1)}, f32[24,1536]{1,0:T(8,128)S(1)}, u32[]{:S(2)}, u32[]{:S(2)}) %collective-permute-start.8) | collective-permute-done | bytes 147488 | tf_op jit(solution)/shard_map/ppermute | solution.py:17
  161.8 0.2 reshape.41
  162.0 0.2 copy.40
  162.1 12.9 %all_to_all.59 = f32[64,8,192]{2,0,1:T(8,128)S(1)} all-to-all(f32[64,8,192]{2,0,1:T(8,128)S(1)} %copy.40), channel_id=1, replica_groups=mesh['amp'=16,'int'=8] {'int'}, dimensions={1} | all-to-all | bytes 786432 | tf_op jit(solution)/shard_map/all_to_all | solution.py:52
  175.1 0.7 divide_add_fusion
  (19 shorter events, 0.2 us)
Async XLA Ops:
  0.0 1.3 slice-start
  0.0 108.9 %collective-permute-start = (bf16[24,96,1536]{2,1,0:T(8,128)(2,1)}, bf16[24,96,1536]{2,1,0:T(8,128)(2,1)}, u32[]{:S(2)}, u32[]{:S(2)}) collective-permute-start(bf16[24,96,1536]{2,1,0:T(8,128)(2,1)} %param.7), channel_id=1, source_target_pairs={{0,8},{8,0},{16,24},{24,16},{32,40},{40,32},{48,56},{56,48},{64,72... | collective-permute-start | bytes 21233672 | tf_op jit(solution)/shard_map/ppermute | solution.py:31
  3.3 28.8 %all-to-all-start.2 = ((bf16[16,384,96]{2,0,1:T(8,128)(2,1)}), bf16[16,384,96]{2,0,1:T(8,128)(2,1)}, u32[]{:S(2)}, u32[]{:S(2)}) async-start(bf16[16,384,96]{2,0,1:T(8,128)(2,1)} %copy.46), calls=%async_computation.2 | async-start | bytes 3145728 | tf_op jit(solution)/shard_map/all_to_all | solution.py:39
  32.1 34.2 %all-to-all-start = ((bf16[24,384,96]{2,0,1:T(8,128)(2,1)}), bf16[24,384,96]{2,0,1:T(8,128)(2,1)S(1)}, u32[]{:S(2)}, u32[]{:S(2)}) async-start(bf16[24,384,96]{2,0,1:T(8,128)(2,1)} %copy.44), calls=%async_computation | async-start | bytes 4718592 | tf_op jit(solution)/shard_map/all_to_all | solution.py:39
  66.2 34.3 %all-to-all-start.1 = ((bf16[24,384,96]{2,0,1:T(8,128)(2,1)}), bf16[24,384,96]{2,0,1:T(8,128)(2,1)}, u32[]{:S(2)}, u32[]{:S(2)}) async-start(bf16[24,384,96]{2,0,1:T(8,128)(2,1)} %copy.45), calls=%async_computation.1 | async-start | bytes 4718592 | tf_op jit(solution)/shard_map/all_to_all | solution.py:39
  100.5 2.5 %copy-start = (bf16[8,24,48,96]{3,1,0,2:T(8,128)(2,1)S(1)}, bf16[8,24,48,96]{3,1,0,2:T(8,128)(2,1)}, u32[]{:S(2)}) copy-start(bf16[8,24,48,96]{3,1,0,2:T(8,128)(2,1)} %copy.31) | copy-start | bytes 5308420
  100.5 6.7 %slice-start.1 = ((s8[7077888]{0:T(1024)(128)(4,1)}), s8[4194304]{0:T(1024)(128)(4,1)S(1)}, s32[]{:S(2)}) async-start(s8[7077888]{0:T(1024)(128)(4,1)} %bitcast.99), calls=%async_computation.5 | async-start | bytes 8388608
  103.0 4.3 %slice-start.2 = ((s8[7077888]{0:T(1024)(128)(4,1)}), s8[2883584]{0:T(1024)(128)(4,1)S(1)}, s32[]{:S(2)}) async-start(s8[7077888]{0:T(1024)(128)(4,1)} %bitcast.99), calls=%async_computation.6 | async-start | bytes 5767168
  108.9 8.8 %copy-start.5 = (f32[128,1536]{1,0:T(8,128)S(1)}, f32[128,1536]{1,0:T(8,128)}, u32[]{:S(2)}) copy-start(f32[128,1536]{1,0:T(8,128)} %convolution_bitcast_fusion.5) | copy-start | bytes 2359300
  113.1 26.9 %collective-permute-start.1 = (f32[2,24,1536]{2,1,0:T(8,128)S(1)}, f32[2,24,1536]{2,1,0:T(8,128)S(1)}, u32[]{:S(2)}, u32[]{:S(2)}) collective-permute-start(f32[2,24,1536]{2,1,0:T(8,128)S(1)} %get-tuple-element.9), channel_id=1, source_target_pairs={{0,16},{8,24},{16,32},{24,40},{32,48},{40,56},{48,0},{56,8},{64,80... | collective-permute-start | bytes 884744 | tf_op jit(solution)/shard_map/ppermute | solution.py:17
  114.7 26.4 %collective-permute-start.2 = (f32[2,24,1536]{2,1,0:T(8,128)S(1)}, f32[2,24,1536]{2,1,0:T(8,128)S(1)}, u32[]{:S(2)}, u32[]{:S(2)}) collective-permute-start(f32[2,24,1536]{2,1,0:T(8,128)S(1)} %get-tuple-element.11), channel_id=1, source_target_pairs={{0,32},{8,40},{16,48},{24,56},{32,0},{40,8},{48,16},{56,24},{64,96... | collective-permute-start | bytes 884744 | tf_op jit(solution)/shard_map/ppermute | solution.py:17
  122.0 14.2 %collective-permute-start.10 = (f32[2,16,1536]{2,1,0:T(8,128)S(1)}, f32[2,16,1536]{2,1,0:T(8,128)S(1)}, u32[]{:S(2)}, u32[]{:S(2)}) collective-permute-start(f32[2,16,1536]{2,1,0:T(8,128)S(1)} %get-tuple-element.17), channel_id=1, source_target_pairs={{0,32},{8,40},{16,48},{24,56},{32,0},{40,8},{48,16},{56,24},{64,96... | collective-permute-start | bytes 589832 | tf_op jit(solution)/shard_map/ppermute | solution.py:17
  122.6 13.6 %collective-permute-start.11 = (f32[2,16,1536]{2,1,0:T(8,128)S(1)}, f32[2,16,1536]{2,1,0:T(8,128)S(1)}, u32[]{:S(2)}, u32[]{:S(2)}) collective-permute-start(f32[2,16,1536]{2,1,0:T(8,128)S(1)} %get-tuple-element.16), channel_id=1, source_target_pairs={{0,48},{8,56},{16,0},{24,8},{32,16},{40,24},{48,32},{56,40},{64,11... | collective-permute-start | bytes 589832 | tf_op jit(solution)/shard_map/ppermute | solution.py:17
  124.3 13.9 %collective-permute-start.9 = (f32[2,16,1536]{2,1,0:T(8,128)S(1)}, f32[2,16,1536]{2,1,0:T(8,128)S(1)}, u32[]{:S(2)}, u32[]{:S(2)}) collective-permute-start(f32[2,16,1536]{2,1,0:T(8,128)S(1)} %get-tuple-element.15), channel_id=1, source_target_pairs={{0,16},{8,24},{16,32},{24,40},{32,48},{40,56},{48,0},{56,8},{64,80... | collective-permute-start | bytes 589832 | tf_op jit(solution)/shard_map/ppermute | solution.py:17
  136.2 9.8 %collective-permute-start.3 = (f32[2,24,1536]{2,1,0:T(8,128)S(1)}, f32[2,24,1536]{2,1,0:T(8,128)S(1)}, u32[]{:S(2)}, u32[]{:S(2)}) collective-permute-start(f32[2,24,1536]{2,1,0:T(8,128)S(1)} %get-tuple-element.10), channel_id=1, source_target_pairs={{0,48},{8,56},{16,0},{24,8},{32,16},{40,24},{48,32},{56,40},{64,11... | collective-permute-start | bytes 884744 | tf_op jit(solution)/shard_map/ppermute | solution.py:17
  136.2 11.0 %collective-permute-start.5 = (f32[2,24,1536]{2,1,0:T(8,128)S(1)}, f32[2,24,1536]{2,1,0:T(8,128)S(1)}, u32[]{:S(2)}, u32[]{:S(2)}) collective-permute-start(f32[2,24,1536]{2,1,0:T(8,128)S(1)} %get-tuple-element.12), channel_id=1, source_target_pairs={{0,16},{8,24},{16,32},{24,40},{32,48},{40,56},{48,0},{56,8},{64,80... | collective-permute-start | bytes 884744 | tf_op jit(solution)/shard_map/ppermute | solution.py:17
  138.2 12.6 %collective-permute-start.6 = (f32[2,24,1536]{2,1,0:T(8,128)S(1)}, f32[2,24,1536]{2,1,0:T(8,128)S(1)}, u32[]{:S(2)}, u32[]{:S(2)}) collective-permute-start(f32[2,24,1536]{2,1,0:T(8,128)S(1)} %get-tuple-element.14), channel_id=1, source_target_pairs={{0,32},{8,40},{16,48},{24,56},{32,0},{40,8},{48,16},{56,24},{64,96... | collective-permute-start | bytes 884744 | tf_op jit(solution)/shard_map/ppermute | solution.py:17
  140.0 14.9 %collective-permute-start.7 = (f32[2,24,1536]{2,1,0:T(8,128)S(1)}, f32[2,24,1536]{2,1,0:T(8,128)S(1)}, u32[]{:S(2)}, u32[]{:S(2)}) collective-permute-start(f32[2,24,1536]{2,1,0:T(8,128)S(1)} %get-tuple-element.13), channel_id=1, source_target_pairs={{0,48},{8,56},{16,0},{24,8},{32,16},{40,24},{48,32},{56,40},{64,11... | collective-permute-start | bytes 884744 | tf_op jit(solution)/shard_map/ppermute | solution.py:17
  141.1 16.0 %collective-permute-start.12 = (f32[16,1536]{1,0:T(8,128)S(1)}, f32[16,1536]{1,0:T(8,128)S(1)}, u32[]{:S(2)}, u32[]{:S(2)}) collective-permute-start(f32[16,1536]{1,0:T(8,128)S(1)} %dynamic-slice_bitcast_fusion.11), channel_id=1, source_target_pairs={{0,64},{8,72},{16,80},{24,88},{32,96},{40,104},{48,112},{56,120},{... | collective-permute-start | bytes 294920 | tf_op jit(solution)/shard_map/ppermute | solution.py:17
  146.1 11.0 %collective-permute-start.4 = (f32[24,1536]{1,0:T(8,128)S(1)}, f32[24,1536]{1,0:T(8,128)S(1)}, u32[]{:S(2)}, u32[]{:S(2)}) collective-permute-start(f32[24,1536]{1,0:T(8,128)S(1)} %dynamic-slice_bitcast_fusion.10), channel_id=1, source_target_pairs={{0,64},{8,72},{16,80},{24,88},{32,96},{40,104},{48,112},{56,120},{... | collective-permute-start | bytes 442376 | tf_op jit(solution)/shard_map/ppermute | solution.py:17
  155.0 6.7 %collective-permute-start.8 = (f32[24,1536]{1,0:T(8,128)S(1)}, f32[24,1536]{1,0:T(8,128)S(1)}, u32[]{:S(2)}, u32[]{:S(2)}) collective-permute-start(f32[24,1536]{1,0:T(8,128)S(1)} %dynamic-slice_bitcast_fusion.9), channel_id=1, source_target_pairs={{0,64},{8,72},{16,80},{24,88},{32,96},{40,104},{48,112},{56,120},{... | collective-permute-start | bytes 442376 | tf_op jit(solution)/shard_map/ppermute | solution.py:17
  157.2 17.9 %copy-start.1 = (f32[64,192]{1,0:T(8,128)S(1)}, f32[64,192]{1,0:T(8,128)}, u32[]{:S(2)}) copy-start(f32[64,192]{1,0:T(8,128)} %param.8) | copy-start | bytes 147460
  157.2 17.9 %copy-start.2 = (f32[64,192]{1,0:T(8,128)S(1)}, f32[64,192]{1,0:T(8,128)}, u32[]{:S(2)}) copy-start(f32[64,192]{1,0:T(8,128)} %param.9) | copy-start | bytes 147460
  157.2 17.9 %copy-start.3 = (f32[192]{0:T(256)S(1)}, f32[192]{0:T(256)}, u32[]{:S(2)}) copy-start(f32[192]{0:T(256)} %param.11) | copy-start | bytes 2308
  157.2 17.9 %copy-start.4 = (f32[64]{0:T(128)S(1)}, f32[64]{0:T(128)}, u32[]{:S(2)}) copy-start(f32[64]{0:T(128)} %param.10) | copy-start | bytes 772

commit v6 on v5

--- a/solution.py
+++ b/solution.py
@@ -3,7 +3,7 @@
 from jax import lax
 from jax.sharding import PartitionSpec as P
 
-SIZES = (24, 24, 16)
+SIZES = (40, 24)
 
 
 def stage_sum(x, me_digit, size, stride, n):

time: 176 us -> 166 us (0.943)
  starting transfers between devices: 35.3 us -> 27.2 us
  matrix products: 23.2 us -> 15.4 us
  waiting for transfers between devices: 81.9 us -> 89.2 us
  local copies, waits for them, and re-layouts: 21.2 us -> 18.2 us
    all_to_all x3 -> x2, starting transfers between devices: 17.4 us -> 12.6 us  [local(): lax.all_to_all(part, 'amp', split_axis=1, concat_axis=0, tiled=True, axis...]
    dot_general x3 -> x2, matrix products: 10.9 us -> 6.51 us  [local(): lax.dot_general(own, integrals, dims, preferred_element_type=jnp.float32)]
    ppermute x12 -> x8, waiting for transfers between devices: 21.9 us -> 26.2 us  [stage_sum(): total = total + lax.ppermute(block, 'amp', perm)]
    dot_general x3 -> x2, matrix products: 12.3 us -> 8.85 us  [local(): lax.dot_general(other, sibling, dims, preferred_element_type=jnp.float32)]
    ppermute x12 -> x8, starting transfers between devices: 17.9 us -> 14.6 us  [stage_sum(): total = total + lax.ppermute(block, 'amp', perm)]
    all_to_all x3 -> x2, waiting for transfers between devices: 60 us -> 63 us  [local(): lax.all_to_all(part, 'amp', split_axis=1, concat_axis=0, tiled=True, axis...]
    slice x3 -> x4, local copies, waits for them, and re-layouts: 4.94 us -> 3.3 us  [local(): part = amplitudes[start:start + size]]
    all_to_all x3 -> x2, local copies, waits for them, and re-layouts: 6.4 us -> 5.21 us  [local(): lax.all_to_all(part, 'amp', split_axis=1, concat_axis=0, tiled=True, axis...]
  transfers between devices with their start and end apart: 16 -> 11, of which waited for: 8 -> 6; matrix products, arithmetic and copies ran while one was open for 22% -> 15% of each run, Pallas kernels for 0% -> 0%
where the time goes in v6:
time: 166 us; the launch traced here: 164 us
  waiting for transfers between devices  89.2 us (54%)
  starting transfers between devices  27.2 us (16%)
  local copies, waits for them, and re-layouts  18.2 us (11%)
  matrix products  15.4 us (9%)
  blocking collectives  12.9 us (8%)
    all_to_all x2, waiting for transfers between devices, local(): lax.all_to_all(part, 'amp', split_axis=1, concat_axis=0, tiled=True, axis...  63 us
    ppermute x8, waiting for transfers between devices, stage_sum(): total = total + lax.ppermute(block, 'amp', perm)  26.2 us
    ppermute x8, starting transfers between devices, stage_sum(): total = total + lax.ppermute(block, 'amp', perm)  14.6 us
    all_to_all x1, blocking collectives, local(): lax.all_to_all(blocks, 'int', split_axis=1, concat_axis=1, tiled=True)  12.9 us
    all_to_all x2, starting transfers between devices, local(): lax.all_to_all(part, 'amp', split_axis=1, concat_axis=0, tiled=True, axis...  12.6 us
    dot_general x2, matrix products, local(): lax.dot_general(other, sibling, dims, preferred_element_type=jnp.float32)  8.85 us
    unnamed x14, local copies, waits for them, and re-layouts  8.48 us
    dot_general x2, matrix products, local(): lax.dot_general(own, integrals, dims, preferred_element_type=jnp.float32)  6.51 us
  transfers between devices with their start and end apart: 11, of which 6 were waited for; matrix products, arithmetic and copies ran while one was open for 15% of the time, Pallas kernels for 0%

profile of v6, /device:TPU:0, one launch (start us, length us, event | category | flops | bytes accessed | tf_op | source)
XLA Modules:
  0.0 164.3 jit_solution(17254788739566403695)
XLA Ops:
  0.0 0.0 slice-start
  0.0 0.0 collective-permute-start
  0.0 1.5 slice-done
  1.5 2.8 %copy.37 = bf16[24,384,96]{2,0,1:T(8,128)(2,1)} copy(bf16[24,384,96]{1,2,0:T(8,128)(2,1)S(1)} %slice-done) | data formatting | bytes 3538944
  4.2 7.9 %all-to-all-start.1 = ((bf16[24,384,96]{2,0,1:T(8,128)(2,1)}), bf16[24,384,96]{2,0,1:T(8,128)(2,1)}, u32[]{:S(2)}, u32[]{:S(2)}) async-start(bf16[24,384,96]{2,0,1:T(8,128)(2,1)} %copy.37), calls=%async_computation.1 | async-start | bytes 4718592 | tf_op jit(solution)/shard_map/all_to_all | solution.py:39
  12.1 0.0 slice-start.1
  12.1 1.8 %slice-done.1 = bf16[40,384,96]{1,2,0:T(8,128)(2,1)S(1)} async-done(((bf16[64,384,96]{1,2,0:T(8,128)(2,1)}), bf16[40,384,96]{1,2,0:T(8,128)(2,1)S(1)}, s32[]{:S(2)}) %slice-start.1) | async-done | bytes 2949144 | tf_op jit(solution)/shard_map/slice | solution.py:37
  13.9 4.5 %copy.34 = bf16[40,384,96]{2,0,1:T(8,128)(2,1)} copy(bf16[40,384,96]{1,2,0:T(8,128)(2,1)S(1)} %slice-done.1) | data formatting | bytes 5898240
  18.4 23.0 %all-to-all-done.1 = bf16[24,384,96]{2,0,1:T(8,128)(2,1)} async-done(((bf16[24,384,96]{2,0,1:T(8,128)(2,1)}), bf16[24,384,96]{2,0,1:T(8,128)(2,1)}, u32[]{:S(2)}, u32[]{:S(2)}) %all-to-all-start.1) | async-done | bytes 1769504 | tf_op jit(solution)/shard_map/all_to_all | solution.py:39
  41.4 4.8 %all-to-all-start = ((bf16[40,384,96]{2,0,1:T(8,128)(2,1)}), bf16[40,384,96]{2,0,1:T(8,128)(2,1)}, u32[]{:S(2)}, u32[]{:S(2)}) async-start(bf16[40,384,96]{2,0,1:T(8,128)(2,1)} %copy.34), calls=%async_computation | async-start | bytes 7864320 | tf_op jit(solution)/shard_map/all_to_all | solution.py:39
  46.2 2.3 %copy.30 = bf16[8,24,48,96]{3,1,0,2:T(8,128)(2,1)S(1)} copy(bf16[8,24,48,96]{3,1,2,0:T(8,128)(2,1)} %bitcast.15) | data formatting | bytes 3538944 | tf_op jit(solution)/shard_map/all_to_all | solution.py:39
  48.5 4.0 %convolution_bitcast_fusion.3 = f32[192,1536]{1,0:T(8,128)S(1)} fusion(bf16[24,96,1536]{2,1,0:T(8,128)(2,1)} %param.7, bf16[192,48,96]{2,0,1:T(8,128)(2,1)S(1)} %bitcast.59, s32[]{:T(128)S(6)} %select_n.79), kind=kOutput, calls=%fused_computation.4 | convolution fusion | flops 1358954496 | bytes 9437188 | tf_op jit(solution)/shard_map/dot_general | solution.py:44
  52.5 40.0 %all-to-all-done = bf16[40,384,96]{2,0,1:T(8,128)(2,1)} async-done(((bf16[40,384,96]{2,0,1:T(8,128)(2,1)}), bf16[40,384,96]{2,0,1:T(8,128)(2,1)}, u32[]{:S(2)}, u32[]{:S(2)}) %all-to-all-start) | async-done | bytes 2949152 | tf_op jit(solution)/shard_map/all_to_all | solution.py:39
  92.5 0.0 slice-start.2
  92.6 2.9 %copy.25 = bf16[8,40,48,96]{3,2,1,0:T(8,128)(2,1)S(1)} copy(bf16[8,40,48,96]{3,1,2,0:T(8,128)(2,1)} %bitcast.2) | data formatting | bytes 5898240 | tf_op jit(solution)/shard_map/all_to_all | solution.py:39
  95.4 0.0 slice-start.3
  95.5 0.7 constant_dynamic-slice_fusion
  96.2 0.0 slice-done.2
  96.2 1.2 slice-done.3
  97.4 2.5 %convolution_bitcast_fusion.1 = f32[320,1536]{1,0:T(8,128)S(1)} fusion(bf16[24,96,1536]{2,1,0:T(8,128)(2,1)S(1)} %bitcast.66, bf16[320,24,96]{2,1,0:T(8,128)(2,1)S(1)} %get-tuple-element.6), kind=kOutput, calls=%fused_computation.1 | convolution fusion | flops 2264924160 | bytes 10518528 | tf_op jit(solution)/shard_map/dot_general | solution.py:44
  99.9 0.0 collective-permute-done
  99.9 4.0 %fusion.1 = f32[192,1536]{1,0:T(8,128)S(1)} fusion(f32[192,1536]{1,0:T(8,128)S(1)} %convolution_bitcast_fusion.3, bf16[24,96,1536]{2,1,0:T(8,128)(2,1)} %collective-permute-done, bf16[192,48,96]{2,0,1:T(8,128)(2,1)S(1)} %bitcast.60, s32[]{:T(128)S(6)} %select_n.80), kind=kOutput, calls=%fused_computation.5 | convolution fusion | flops 1359249408 | bytes 10616836 | tf_op jit(solution)/shard_map/dot_general | solution.py:45
  103.9 0.1 dynamic-slice_bitcast_fusion.5
  104.0 1.6 collective-permute-start.5
  105.6 3.0 %collective-permute-start.6 = (f32[2,24,1536]{2,1,0:T(8,128)S(1)}, f32[2,24,1536]{2,1,0:T(8,128)S(1)}, u32[]{:S(2)}, u32[]{:S(2)}) collective-permute-start(f32[2,24,1536]{2,1,0:T(8,128)S(1)} %get-tuple-element.12), channel_id=1, source_target_pairs={{0,32},{8,40},{16,48},{24,56},{32,0},{40,8},{48,16},{56,24},{64,96... | collective-permute-start | bytes 884744 | tf_op jit(solution)/shard_map/ppermute | solution.py:17
  108.6 1.1 collective-permute-start.7
  109.7 4.8 %fusion = f32[320,1536]{1,0:T(8,128)S(1)} fusion(f32[320,1536]{1,0:T(8,128)S(1)} %convolution_bitcast_fusion.1, bf16[24,96,1536]{2,1,0:T(8,128)(2,1)} %collective-permute-done, bf16[320,24,96]{2,1,0:T(8,128)(2,1)S(1)} %get-tuple-element.5), kind=kOutput, calls=%fused_computation.2 | convolution fusion | flops 2265415680 | bytes 12484608 | tf_op jit(solution)/shard_map/dot_general | solution.py:45
  114.5 0.1 dynamic-slice_bitcast_fusion.2
  114.6 1.0 collective-permute-start.1
  115.6 0.6 collective-permute-start.2
  116.2 0.0 collective-permute-done.5
  116.2 2.2 %collective-permute-start.3 = (f32[2,40,1536]{2,1,0:T(8,128)S(1)}, f32[2,40,1536]{2,1,0:T(8,128)S(1)}, u32[]{:S(2)}, u32[]{:S(2)}) collective-permute-start(f32[2,40,1536]{2,1,0:T(8,128)S(1)} %get-tuple-element.8), channel_id=1, source_target_pairs={{0,48},{8,56},{16,0},{24,8},{32,16},{40,24},{48,32},{56,40},{64,11... | collective-permute-start | bytes 1474568 | tf_op jit(solution)/shard_map/ppermute | solution.py:17
  118.4 4.5 %collective-permute-done.6 = f32[2,24,1536]{2,1,0:T(8,128)S(1)} collective-permute-done((f32[2,24,1536]{2,1,0:T(8,128)S(1)}, f32[2,24,1536]{2,1,0:T(8,128)S(1)}, u32[]{:S(2)}, u32[]{:S(2)}) %collective-permute-start.6) | collective-permute-done | bytes 294944 | tf_op jit(solution)/shard_map/ppermute | solution.py:17
  122.8 0.0 collective-permute-done.7
  122.8 0.1 fusion.9
  122.9 2.3 %collective-permute-start.8 = (f32[24,1536]{1,0:T(8,128)S(1)}, f32[24,1536]{1,0:T(8,128)S(1)}, u32[]{:S(2)}, u32[]{:S(2)}) collective-permute-start(f32[24,1536]{1,0:T(8,128)S(1)} %dynamic-slice_bitcast_fusion.7), channel_id=1, source_target_pairs={{0,64},{8,72},{16,80},{24,88},{32,96},{40,104},{48,112},{56,120},{... | collective-permute-start | bytes 442376 | tf_op jit(solution)/shard_map/ppermute | solution.py:17
  125.2 8.0 %collective-permute-done.1 = f32[2,40,1536]{2,1,0:T(8,128)S(1)} collective-permute-done((f32[2,40,1536]{2,1,0:T(8,128)S(1)}, f32[2,40,1536]{2,1,0:T(8,128)S(1)}, u32[]{:S(2)}, u32[]{:S(2)}) %collective-permute-start.1) | collective-permute-done | bytes 491552 | tf_op jit(solution)/shard_map/ppermute | solution.py:17
  133.3 8.4 %collective-permute-done.2 = f32[2,40,1536]{2,1,0:T(8,128)S(1)} collective-permute-done((f32[2,40,1536]{2,1,0:T(8,128)S(1)}, f32[2,40,1536]{2,1,0:T(8,128)S(1)}, u32[]{:S(2)}, u32[]{:S(2)}) %collective-permute-start.2) | collective-permute-done | bytes 491552 | tf_op jit(solution)/shard_map/ppermute | solution.py:17
  141.7 0.0 collective-permute-done.3
  141.7 0.1 fusion.7
  141.8 2.9 %collective-permute-start.4 = (f32[40,1536]{1,0:T(8,128)S(1)}, f32[40,1536]{1,0:T(8,128)S(1)}, u32[]{:S(2)}, u32[]{:S(2)}) collective-permute-start(f32[40,1536]{1,0:T(8,128)S(1)} %dynamic-slice_bitcast_fusion.6), channel_id=1, source_target_pairs={{0,64},{8,72},{16,80},{24,88},{32,96},{40,104},{48,112},{56,120},{... | collective-permute-start | bytes 737288 | tf_op jit(solution)/shard_map/ppermute | solution.py:17
  144.8 0.0 collective-permute-done.8
  144.8 5.3 %collective-permute-done.4 = f32[40,1536]{1,0:T(8,128)S(1)} collective-permute-done((f32[40,1536]{1,0:T(8,128)S(1)}, f32[40,1536]{1,0:T(8,128)S(1)}, u32[]{:S(2)}, u32[]{:S(2)}) %collective-permute-start.4) | collective-permute-done | bytes 245792 | tf_op jit(solution)/shard_map/ppermute | solution.py:17
  150.1 0.0 copy-start
  150.1 0.0 copy-start.1
  150.2 0.0 copy-start.2
  150.2 0.0 copy-start.3
  150.2 0.2 reshape.29
  150.3 0.2 copy.31
  150.5 12.9 %all_to_all.41 = f32[64,8,192]{2,0,1:T(8,128)S(1)} all-to-all(f32[64,8,192]{2,0,1:T(8,128)S(1)} %copy.31), channel_id=1, replica_groups=mesh['amp'=16,'int'=8] {'int'}, dimensions={1} | all-to-all | bytes 786432 | tf_op jit(solution)/shard_map/all_to_all | solution.py:52
  163.5 0.0 copy-done
  163.5 0.0 copy-done.1
  163.5 0.0 copy-done.2
  163.5 0.0 copy-done.3
  163.6 0.7 divide_add_fusion
  (7 shorter events, 0.2 us)
Async XLA Ops:
  0.0 1.5 slice-start
  0.0 99.9 %collective-permute-start = (bf16[24,96,1536]{2,1,0:T(8,128)(2,1)}, bf16[24,96,1536]{2,1,0:T(8,128)(2,1)}, u32[]{:S(2)}, u32[]{:S(2)}) collective-permute-start(bf16[24,96,1536]{2,1,0:T(8,128)(2,1)} %param.7), channel_id=1, source_target_pairs={{0,8},{8,0},{16,24},{24,16},{32,40},{40,32},{48,56},{56,48},{64,72... | collective-permute-start | bytes 21233672 | tf_op jit(solution)/shard_map/ppermute | solution.py:31
  4.2 37.2 %all-to-all-start.1 = ((bf16[24,384,96]{2,0,1:T(8,128)(2,1)}), bf16[24,384,96]{2,0,1:T(8,128)(2,1)}, u32[]{:S(2)}, u32[]{:S(2)}) async-start(bf16[24,384,96]{2,0,1:T(8,128)(2,1)} %copy.37), calls=%async_computation.1 | async-start | bytes 4718592 | tf_op jit(solution)/shard_map/all_to_all | solution.py:39
  12.1 1.8 %slice-start.1 = ((bf16[64,384,96]{1,2,0:T(8,128)(2,1)}), bf16[40,384,96]{1,2,0:T(8,128)(2,1)S(1)}, s32[]{:S(2)}) async-start(bf16[64,384,96]{1,2,0:T(8,128)(2,1)} %param.6), calls=%async_computation.4 | async-start | bytes 5898240 | tf_op jit(solution)/shard_map/slice | solution.py:37
  41.4 51.1 %all-to-all-start = ((bf16[40,384,96]{2,0,1:T(8,128)(2,1)}), bf16[40,384,96]{2,0,1:T(8,128)(2,1)}, u32[]{:S(2)}, u32[]{:S(2)}) async-start(bf16[40,384,96]{2,0,1:T(8,128)(2,1)} %copy.34), calls=%async_computation | async-start | bytes 7864320 | tf_op jit(solution)/shard_map/all_to_all | solution.py:39
  92.5 3.6 %slice-start.2 = ((s8[7077888]{0:T(1024)(128)(4,1)}), s8[4194304]{0:T(1024)(128)(4,1)S(1)}, s32[]{:S(2)}) async-start(s8[7077888]{0:T(1024)(128)(4,1)} %bitcast.65), calls=%async_computation.5 | async-start | bytes 8388608
  95.4 1.9 %slice-start.3 = ((s8[7077888]{0:T(1024)(128)(4,1)}), s8[2883584]{0:T(1024)(128)(4,1)S(1)}, s32[]{:S(2)}) async-start(s8[7077888]{0:T(1024)(128)(4,1)} %bitcast.65), calls=%async_computation.6 | async-start | bytes 5767168
  104.0 12.2 %collective-permute-start.5 = (f32[2,24,1536]{2,1,0:T(8,128)S(1)}, f32[2,24,1536]{2,1,0:T(8,128)S(1)}, u32[]{:S(2)}, u32[]{:S(2)}) collective-permute-start(f32[2,24,1536]{2,1,0:T(8,128)S(1)} %get-tuple-element.10), channel_id=1, source_target_pairs={{0,16},{8,24},{16,32},{24,40},{32,48},{40,56},{48,0},{56,8},{64,80... | collective-permute-start | bytes 884744 | tf_op jit(solution)/shard_map/ppermute | solution.py:17
  105.6 17.2 %collective-permute-start.6 = (f32[2,24,1536]{2,1,0:T(8,128)S(1)}, f32[2,24,1536]{2,1,0:T(8,128)S(1)}, u32[]{:S(2)}, u32[]{:S(2)}) collective-permute-start(f32[2,24,1536]{2,1,0:T(8,128)S(1)} %get-tuple-element.12), channel_id=1, source_target_pairs={{0,32},{8,40},{16,48},{24,56},{32,0},{40,8},{48,16},{56,24},{64,96... | collective-permute-start | bytes 884744 | tf_op jit(solution)/shard_map/ppermute | solution.py:17
  108.6 14.3 %collective-permute-start.7 = (f32[2,24,1536]{2,1,0:T(8,128)S(1)}, f32[2,24,1536]{2,1,0:T(8,128)S(1)}, u32[]{:S(2)}, u32[]{:S(2)}) collective-permute-start(f32[2,24,1536]{2,1,0:T(8,128)S(1)} %get-tuple-element.11), channel_id=1, source_target_pairs={{0,48},{8,56},{16,0},{24,8},{32,16},{40,24},{48,32},{56,40},{64,11... | collective-permute-start | bytes 884744 | tf_op jit(solution)/shard_map/ppermute | solution.py:17
  114.6 18.6 %collective-permute-start.1 = (f32[2,40,1536]{2,1,0:T(8,128)S(1)}, f32[2,40,1536]{2,1,0:T(8,128)S(1)}, u32[]{:S(2)}, u32[]{:S(2)}) collective-permute-start(f32[2,40,1536]{2,1,0:T(8,128)S(1)} %get-tuple-element.7), channel_id=1, source_target_pairs={{0,16},{8,24},{16,32},{24,40},{32,48},{40,56},{48,0},{56,8},{64,80... | collective-permute-start | bytes 1474568 | tf_op jit(solution)/shard_map/ppermute | solution.py:17
  115.6 26.1 %collective-permute-start.2 = (f32[2,40,1536]{2,1,0:T(8,128)S(1)}, f32[2,40,1536]{2,1,0:T(8,128)S(1)}, u32[]{:S(2)}, u32[]{:S(2)}) collective-permute-start(f32[2,40,1536]{2,1,0:T(8,128)S(1)} %get-tuple-element.9), channel_id=1, source_target_pairs={{0,32},{8,40},{16,48},{24,56},{32,0},{40,8},{48,16},{56,24},{64,96... | collective-permute-start | bytes 1474568 | tf_op jit(solution)/shard_map/ppermute | solution.py:17
  116.2 25.5 %collective-permute-start.3 = (f32[2,40,1536]{2,1,0:T(8,128)S(1)}, f32[2,40,1536]{2,1,0:T(8,128)S(1)}, u32[]{:S(2)}, u32[]{:S(2)}) collective-permute-start(f32[2,40,1536]{2,1,0:T(8,128)S(1)} %get-tuple-element.8), channel_id=1, source_target_pairs={{0,48},{8,56},{16,0},{24,8},{32,16},{40,24},{48,32},{56,40},{64,11... | collective-permute-start | bytes 1474568 | tf_op jit(solution)/shard_map/ppermute | solution.py:17
  122.9 21.8 %collective-permute-start.8 = (f32[24,1536]{1,0:T(8,128)S(1)}, f32[24,1536]{1,0:T(8,128)S(1)}, u32[]{:S(2)}, u32[]{:S(2)}) collective-permute-start(f32[24,1536]{1,0:T(8,128)S(1)} %dynamic-slice_bitcast_fusion.7), channel_id=1, source_target_pairs={{0,64},{8,72},{16,80},{24,88},{32,96},{40,104},{48,112},{56,120},{... | collective-permute-start | bytes 442376 | tf_op jit(solution)/shard_map/ppermute | solution.py:17
  141.8 8.2 %collective-permute-start.4 = (f32[40,1536]{1,0:T(8,128)S(1)}, f32[40,1536]{1,0:T(8,128)S(1)}, u32[]{:S(2)}, u32[]{:S(2)}) collective-permute-start(f32[40,1536]{1,0:T(8,128)S(1)} %dynamic-slice_bitcast_fusion.6), channel_id=1, source_target_pairs={{0,64},{8,72},{16,80},{24,88},{32,96},{40,104},{48,112},{56,120},{... | collective-permute-start | bytes 737288 | tf_op jit(solution)/shard_map/ppermute | solution.py:17
  150.1 13.4 %copy-start = (f32[64,192]{1,0:T(8,128)S(1)}, f32[64,192]{1,0:T(8,128)}, u32[]{:S(2)}) copy-start(f32[64,192]{1,0:T(8,128)} %param.8) | copy-start | bytes 147460
  150.1 13.4 %copy-start.1 = (f32[64,192]{1,0:T(8,128)S(1)}, f32[64,192]{1,0:T(8,128)}, u32[]{:S(2)}) copy-start(f32[64,192]{1,0:T(8,128)} %param.9) | copy-start | bytes 147460
  150.2 13.4 %copy-start.2 = (f32[192]{0:T(256)S(1)}, f32[192]{0:T(256)}, u32[]{:S(2)}) copy-start(f32[192]{0:T(256)} %param.11) | copy-start | bytes 2308
  150.2 13.4 %copy-start.3 = (f32[64]{0:T(128)S(1)}, f32[64]{0:T(128)}, u32[]{:S(2)}) copy-start(f32[64]{0:T(128)} %param.10) | copy-start | bytes 772

commit v7 on v6

--- a/solution.py
+++ b/solution.py
@@ -33,19 +33,26 @@
     dims = (((1, 2), (0, 1)), ((), ()))
     pieces = []
     start = 0
+    def reduce(partial):
+        x = partial.reshape(n_hi, n_z, -1, partial.shape[-1])
+        x = stage_sum(jnp.moveaxis(x, 1, 0), z, n_z, n_core, n)
+        return stage_sum(x, hi, n_hi, n_core * n_z, n)
+
+    prev = None
     for size in SIZES:
         part = amplitudes[start:start + size]
         start += size
+        if prev is not None:
+            prev, part = lax.optimization_barrier((prev, part))
+            pieces.append(reduce(prev))
         got = lax.all_to_all(
             part, "amp", split_axis=1, concat_axis=0, tiled=True, axis_index_groups=groups
         )
         own = lax.dynamic_slice_in_dim(got, core * width, width, axis=1)
         other = lax.dynamic_slice_in_dim(got, (1 - core) * width, width, axis=1)
         partial = lax.dot_general(own, integrals, dims, preferred_element_type=jnp.float32)
-        partial = partial + lax.dot_general(other, sibling, dims, preferred_element_type=jnp.float32)
-        x = partial.reshape(n_hi, n_z, size, -1)
-        x = stage_sum(jnp.moveaxis(x, 1, 0), z, n_z, n_core, n)
-        pieces.append(stage_sum(x, hi, n_hi, n_core * n_z, n))
+        prev = partial + lax.dot_general(other, sibling, dims, preferred_element_type=jnp.float32)
+    pieces.append(reduce(prev))
     rows = jnp.concatenate(pieces, axis=0)
     n_int = lax.axis_size("int")
     blocks = rows.reshape(rows.shape[0], n_int, -1)

time: 166 us -> 164 us (0.988)
  waiting for transfers between devices: 89.2 us -> 73.3 us
  starting transfers between devices: 27.2 us -> 38.4 us
  matrix products: 15.4 us -> 17.5 us
    ppermute x8, waiting for transfers between devices: 26.2 us -> 10.4 us  [stage_sum(): total = total + lax.ppermute(block, 'amp', perm)]
    ppermute x8, starting transfers between devices: 14.6 us -> 25.7 us  [stage_sum(): total = total + lax.ppermute(block, 'amp', perm)]
    unnamed x14 -> x13, local copies, waits for them, and re-layouts: 8.48 us -> 5.52 us
    optimization_barrier x0 -> x1, local copies, waits for them, and re-layouts: none -> 2.73 us  [local(): prev, part = lax.optimization_barrier((prev, part))]
    squeeze x4, local copies, waits for them, and re-layouts: 0.23 us -> 2.5 us  [stage_sum(): lax.dynamic_index_in_dim(x, (me_digit + s) % size, 0, keepdims=False)]
    dot_general x2, matrix products: 8.85 us -> 10.9 us  [local(): lax.dot_general(other, sibling, dims, preferred_element_type=jnp.float32)]
    all_to_all x2, local copies, waits for them, and re-layouts: 5.21 us -> 3.55 us  [local(): lax.all_to_all(part, 'amp', split_axis=1, concat_axis=0, tiled=True, axis...]
  transfers between devices with their start and end apart: 11 -> 11, of which waited for: 6 -> 5; matrix products, arithmetic and copies ran while one was open for 15% -> 16% of each run, Pallas kernels for 0% -> 0%
where the time goes in v7:
time: 164 us; the launch traced here: 163 us
  waiting for transfers between devices  73.3 us (45%)
  starting transfers between devices  38.4 us (23%)
  local copies, waits for them, and re-layouts  18.6 us (11%)
  matrix products  17.5 us (11%)
  blocking collectives  12.9 us (8%)
  other arithmetic  2.33 us (1%)
    all_to_all x2, waiting for transfers between devices, local(): lax.all_to_all(part, 'amp', split_axis=1, concat_axis=0, tiled=True, axis...  62.9 us
    ppermute x8, starting transfers between devices, stage_sum(): total = total + lax.ppermute(block, 'amp', perm)  25.7 us
    all_to_all x1, blocking collectives, local(): lax.all_to_all(blocks, 'int', split_axis=1, concat_axis=1, tiled=True)  12.9 us
    all_to_all x2, starting transfers between devices, local(): lax.all_to_all(part, 'amp', split_axis=1, concat_axis=0, tiled=True, axis...  12.6 us
    dot_general x2, matrix products, local(): lax.dot_general(other, sibling, dims, preferred_element_type=jnp.float32)  10.9 us
    ppermute x8, waiting for transfers between devices, stage_sum(): total = total + lax.ppermute(block, 'amp', perm)  10.4 us
    dot_general x2, matrix products, local(): lax.dot_general(own, integrals, dims, preferred_element_type=jnp.float32)  6.53 us
    unnamed x13, local copies, waits for them, and re-layouts  5.52 us
  transfers between devices with their start and end apart: 11, of which 5 were waited for; matrix products, arithmetic and copies ran while one was open for 16% of the time, Pallas kernels for 0%

profile of v7, /device:TPU:0, one launch (start us, length us, event | category | flops | bytes accessed | tf_op | source)
XLA Modules:
  0.0 163.3 jit_solution(9667660021959236303)
XLA Ops:
  0.0 0.0 slice-start
  0.0 0.0 collective-permute-start
  0.0 1.8 %slice-done = bf16[40,384,96]{1,2,0:T(8,128)(2,1)S(1)} async-done(((bf16[64,384,96]{1,2,0:T(8,128)(2,1)}), bf16[40,384,96]{1,2,0:T(8,128)(2,1)S(1)}, s32[]{:S(2)}) %slice-start) | async-done | bytes 2949144 | tf_op jit(solution)/shard_map/slice | solution.py:43
  1.8 4.3 %copy.34 = bf16[40,384,96]{2,0,1:T(8,128)(2,1)} copy(bf16[40,384,96]{1,2,0:T(8,128)(2,1)S(1)} %slice-done) | data formatting | bytes 5898240
  6.1 7.9 %all-to-all-start = ((bf16[40,384,96]{2,0,1:T(8,128)(2,1)}), bf16[40,384,96]{2,0,1:T(8,128)(2,1)}, u32[]{:S(2)}, u32[]{:S(2)}) async-start(bf16[40,384,96]{2,0,1:T(8,128)(2,1)} %copy.34), calls=%async_computation | async-start | bytes 7864320 | tf_op jit(solution)/shard_map/all_to_all | solution.py:48
  14.0 0.0 slice-start.1
  14.0 1.4 slice-done.1
  15.4 2.7 %copy.37 = bf16[24,384,96]{2,0,1:T(8,128)(2,1)} copy(bf16[24,384,96]{1,2,0:T(8,128)(2,1)S(1)} %slice-done.1) | data formatting | bytes 3538944 | tf_op jit(solution)/shard_map/optimization_barrier | solution.py:46
  18.2 42.0 %all-to-all-done = bf16[40,384,96]{2,0,1:T(8,128)(2,1)} async-done(((bf16[40,384,96]{2,0,1:T(8,128)(2,1)}), bf16[40,384,96]{2,0,1:T(8,128)(2,1)}, u32[]{:S(2)}, u32[]{:S(2)}) %all-to-all-start) | async-done | bytes 2949152 | tf_op jit(solution)/shard_map/all_to_all | solution.py:48
  60.1 0.0 slice-start.2
  60.1 2.9 %copy.25 = bf16[8,40,48,96]{3,2,1,0:T(8,128)(2,1)S(1)} copy(bf16[8,40,48,96]{3,1,2,0:T(8,128)(2,1)} %bitcast.2) | data formatting | bytes 5898240 | tf_op jit(solution)/shard_map/all_to_all | solution.py:48
  63.0 0.0 slice-start.3
  63.1 0.7 constant_dynamic-slice_fusion
  63.7 0.0 slice-done.2
  63.8 1.2 slice-done.3
  65.0 2.5 %convolution_bitcast_fusion.1 = f32[320,1536]{1,0:T(8,128)S(1)} fusion(bf16[24,96,1536]{2,1,0:T(8,128)(2,1)S(1)} %bitcast.67, bf16[320,24,96]{2,1,0:T(8,128)(2,1)S(1)} %get-tuple-element.10), kind=kOutput, calls=%fused_computation.1 | convolution fusion | flops 2264924160 | bytes 10518528 | tf_op jit(solution)/shard_map/dot_general | solution.py:53
  67.5 0.0 collective-permute-done
  67.5 6.9 %fusion = f32[320,1536]{1,0:T(8,128)} fusion(f32[320,1536]{1,0:T(8,128)S(1)} %convolution_bitcast_fusion.1, bf16[24,96,1536]{2,1,0:T(8,128)(2,1)} %collective-permute-done, bf16[320,24,96]{2,1,0:T(8,128)(2,1)S(1)} %get-tuple-element.9), kind=kOutput, calls=%fused_computation.2 | convolution fusion | flops 2265415680 | bytes 12484608 | tf_op jit(solution)/shard_map/dot_general | solution.py:54
  74.4 4.8 %all-to-all-start.1 = ((bf16[24,384,96]{2,0,1:T(8,128)(2,1)}), bf16[24,384,96]{2,0,1:T(8,128)(2,1)S(1)}, u32[]{:S(2)}, u32[]{:S(2)}) async-start(bf16[24,384,96]{2,0,1:T(8,128)(2,1)} %copy.37), calls=%async_computation.1 | async-start | bytes 4718592 | tf_op jit(solution)/shard_map/all_to_all | solution.py:48
  79.1 2.4 %dynamic-slice_bitcast_fusion.2 = (f32[2,40,1536]{2,1,0:T(8,128)}, f32[2,40,1536]{2,1,0:T(8,128)S(1)}, f32[2,40,1536]{2,1,0:T(8,128)}) fusion(f32[2,4,40,1536]{3,2,1,0:T(8,128)} %bitcast.62, s32[]{:T(128)S(6)} %select_n.85, s32[]{:T(128)S(6)} %select_n.89, s32[]{:T(128)S(6)} %select_n.87), kind=kLoop, calls=%fused_computation.15 | loop fusion | bytes 2949132 | tf_op jit(solution)/shard_map/jit(dynamic_index_in_dim)/squeeze | solution.py:12
  81.5 2.0 %collective-permute-start.1 = (f32[2,40,1536]{2,1,0:T(8,128)}, f32[2,40,1536]{2,1,0:T(8,128)S(1)}, u32[]{:S(2)}, u32[]{:S(2)}) collective-permute-start(f32[2,40,1536]{2,1,0:T(8,128)} %get-tuple-element.11), channel_id=1, source_target_pairs={{0,16},{8,24},{16,32},{24,40},{32,48},{40,56},{48,0},{56,8},{64,80... | collective-permute-start | bytes 1474568 | tf_op jit(solution)/shard_map/ppermute | solution.py:17
  83.5 2.7 %collective-permute-start.2 = (f32[2,40,1536]{2,1,0:T(8,128)}, f32[2,40,1536]{2,1,0:T(8,128)}, u32[]{:S(2)}, u32[]{:S(2)}) collective-permute-start(f32[2,40,1536]{2,1,0:T(8,128)} %get-tuple-element.13), channel_id=1, source_target_pairs={{0,32},{8,40},{16,48},{24,56},{32,0},{40,8},{48,16},{56,24},{64,96... | collective-permute-start | bytes 1474568 | tf_op jit(solution)/shard_map/ppermute | solution.py:17
  86.2 1.5 collective-permute-start.3
  87.7 20.9 %all-to-all-done.1 = bf16[24,384,96]{2,0,1:T(8,128)(2,1)S(1)} async-done(((bf16[24,384,96]{2,0,1:T(8,128)(2,1)}), bf16[24,384,96]{2,0,1:T(8,128)(2,1)S(1)}, u32[]{:S(2)}, u32[]{:S(2)}) %all-to-all-start.1) | async-done | bytes 1769504 | tf_op jit(solution)/shard_map/all_to_all | solution.py:48
  108.6 0.7 copy.30
  109.2 4.0 %convolution_bitcast_fusion.3 = f32[192,1536]{1,0:T(8,128)S(1)} fusion(bf16[24,96,1536]{2,1,0:T(8,128)(2,1)} %param.7, bf16[192,48,96]{2,0,1:T(8,128)(2,1)S(1)} %bitcast.60, s32[]{:T(128)S(6)} %select_n.79), kind=kOutput, calls=%fused_computation.4 | convolution fusion | flops 1358954496 | bytes 9437188 | tf_op jit(solution)/shard_map/dot_general | solution.py:53
  113.3 4.1 %fusion.1 = f32[192,1536]{1,0:T(8,128)S(1)} fusion(f32[192,1536]{1,0:T(8,128)S(1)} %convolution_bitcast_fusion.3, bf16[24,96,1536]{2,1,0:T(8,128)(2,1)} %collective-permute-done, bf16[192,48,96]{2,0,1:T(8,128)(2,1)S(1)} %bitcast.61, s32[]{:T(128)S(6)} %select_n.80), kind=kOutput, calls=%fused_computation.5 | convolution fusion | flops 1359249408 | bytes 10616836 | tf_op jit(solution)/shard_map/dot_general | solution.py:54
  117.3 0.1 dynamic-slice_bitcast_fusion.5
  117.4 11.0 %collective-permute-start.5 = (f32[2,24,1536]{2,1,0:T(8,128)S(1)}, f32[2,24,1536]{2,1,0:T(8,128)S(1)}, u32[]{:S(2)}, u32[]{:S(2)}) collective-permute-start(f32[2,24,1536]{2,1,0:T(8,128)S(1)} %get-tuple-element.14), channel_id=1, source_target_pairs={{0,16},{8,24},{16,32},{24,40},{32,48},{40,56},{48,0},{56,8},{64,80... | collective-permute-start | bytes 884744 | tf_op jit(solution)/shard_map/ppermute | solution.py:17
  128.5 0.0 collective-permute-start.6
  128.5 0.0 collective-permute-done.1
  128.5 2.8 %collective-permute-start.7 = (f32[2,24,1536]{2,1,0:T(8,128)S(1)}, f32[2,24,1536]{2,1,0:T(8,128)S(1)}, u32[]{:S(2)}, u32[]{:S(2)}) collective-permute-start(f32[2,24,1536]{2,1,0:T(8,128)S(1)} %get-tuple-element.15), channel_id=1, source_target_pairs={{0,48},{8,56},{16,0},{24,8},{32,16},{40,24},{48,32},{56,40},{64,11... | collective-permute-start | bytes 884744 | tf_op jit(solution)/shard_map/ppermute | solution.py:17
  131.2 0.0 collective-permute-done.2
  131.2 0.0 collective-permute-done.3
  131.2 1.4 fusion.7
  132.7 2.7 %collective-permute-start.4 = (f32[40,1536]{1,0:T(8,128)S(1)}, f32[40,1536]{1,0:T(8,128)S(1)}, u32[]{:S(2)}, u32[]{:S(2)}) collective-permute-start(f32[40,1536]{1,0:T(8,128)S(1)} %dynamic-slice_bitcast_fusion.6), channel_id=1, source_target_pairs={{0,64},{8,72},{16,80},{24,88},{32,96},{40,104},{48,112},{56,120},{... | collective-permute-start | bytes 737288 | tf_op jit(solution)/shard_map/ppermute | solution.py:17
  135.4 1.6 collective-permute-done.5
  137.1 5.2 %collective-permute-done.6 = f32[2,24,1536]{2,1,0:T(8,128)S(1)} collective-permute-done((f32[2,24,1536]{2,1,0:T(8,128)S(1)}, f32[2,24,1536]{2,1,0:T(8,128)S(1)}, u32[]{:S(2)}, u32[]{:S(2)}) %collective-permute-start.6) | collective-permute-done | bytes 294944 | tf_op jit(solution)/shard_map/ppermute | solution.py:17
  142.2 0.0 collective-permute-done.7
  142.2 0.1 fusion.9
  142.3 3.0 %collective-permute-start.8 = (f32[24,1536]{1,0:T(8,128)S(1)}, f32[24,1536]{1,0:T(8,128)S(1)}, u32[]{:S(2)}, u32[]{:S(2)}) collective-permute-start(f32[24,1536]{1,0:T(8,128)S(1)} %dynamic-slice_bitcast_fusion.7), channel_id=1, source_target_pairs={{0,64},{8,72},{16,80},{24,88},{32,96},{40,104},{48,112},{56,120},{... | collective-permute-start | bytes 442376 | tf_op jit(solution)/shard_map/ppermute | solution.py:17
  145.4 0.0 collective-permute-done.4
  145.4 3.6 %collective-permute-done.8 = f32[24,1536]{1,0:T(8,128)S(1)} collective-permute-done((f32[24,1536]{1,0:T(8,128)S(1)}, f32[24,1536]{1,0:T(8,128)S(1)}, u32[]{:S(2)}, u32[]{:S(2)}) %collective-permute-start.8) | collective-permute-done | bytes 147488 | tf_op jit(solution)/shard_map/ppermute | solution.py:17
  149.1 0.0 copy-start
  149.1 0.0 copy-start.1
  149.1 0.0 copy-start.2
  149.2 0.0 copy-start.3
  149.2 0.2 reshape.29
  149.3 0.2 copy.31
  149.5 12.9 %all_to_all.41 = f32[64,8,192]{2,0,1:T(8,128)S(1)} all-to-all(f32[64,8,192]{2,0,1:T(8,128)S(1)} %copy.31), channel_id=1, replica_groups=mesh['amp'=16,'int'=8] {'int'}, dimensions={1} | all-to-all | bytes 786432 | tf_op jit(solution)/shard_map/all_to_all | solution.py:59
  162.5 0.0 copy-done
  162.5 0.0 copy-done.1
  162.5 0.0 copy-done.2
  162.5 0.0 copy-done.3
  162.5 0.7 divide_add_fusion
  (7 shorter events, 0.2 us)
Async XLA Ops:
  0.0 1.8 %slice-start = ((bf16[64,384,96]{1,2,0:T(8,128)(2,1)}), bf16[40,384,96]{1,2,0:T(8,128)(2,1)S(1)}, s32[]{:S(2)}) async-start(bf16[64,384,96]{1,2,0:T(8,128)(2,1)} %param.6), calls=%async_computation.3 | async-start | bytes 5898240 | tf_op jit(solution)/shard_map/slice | solution.py:43
  0.0 67.5 %collective-permute-start = (bf16[24,96,1536]{2,1,0:T(8,128)(2,1)}, bf16[24,96,1536]{2,1,0:T(8,128)(2,1)}, u32[]{:S(2)}, u32[]{:S(2)}) collective-permute-start(bf16[24,96,1536]{2,1,0:T(8,128)(2,1)} %param.7), channel_id=1, source_target_pairs={{0,8},{8,0},{16,24},{24,16},{32,40},{40,32},{48,56},{56,48},{64,72... | collective-permute-start | bytes 21233672 | tf_op jit(solution)/shard_map/ppermute | solution.py:31
  6.1 54.0 %all-to-all-start = ((bf16[40,384,96]{2,0,1:T(8,128)(2,1)}), bf16[40,384,96]{2,0,1:T(8,128)(2,1)}, u32[]{:S(2)}, u32[]{:S(2)}) async-start(bf16[40,384,96]{2,0,1:T(8,128)(2,1)} %copy.34), calls=%async_computation | async-start | bytes 7864320 | tf_op jit(solution)/shard_map/all_to_all | solution.py:48
  14.0 1.5 slice-start.1
  60.1 3.6 %slice-start.2 = ((s8[7077888]{0:T(1024)(128)(4,1)}), s8[4194304]{0:T(1024)(128)(4,1)S(1)}, s32[]{:S(2)}) async-start(s8[7077888]{0:T(1024)(128)(4,1)} %bitcast.66), calls=%async_computation.5 | async-start | bytes 8388608
  63.0 1.9 %slice-start.3 = ((s8[7077888]{0:T(1024)(128)(4,1)}), s8[2883584]{0:T(1024)(128)(4,1)S(1)}, s32[]{:S(2)}) async-start(s8[7077888]{0:T(1024)(128)(4,1)} %bitcast.66), calls=%async_computation.6 | async-start | bytes 5767168
  74.4 34.2 %all-to-all-start.1 = ((bf16[24,384,96]{2,0,1:T(8,128)(2,1)}), bf16[24,384,96]{2,0,1:T(8,128)(2,1)S(1)}, u32[]{:S(2)}, u32[]{:S(2)}) async-start(bf16[24,384,96]{2,0,1:T(8,128)(2,1)} %copy.37), calls=%async_computation.1 | async-start | bytes 4718592 | tf_op jit(solution)/shard_map/all_to_all | solution.py:48
  81.5 47.0 %collective-permute-start.1 = (f32[2,40,1536]{2,1,0:T(8,128)}, f32[2,40,1536]{2,1,0:T(8,128)S(1)}, u32[]{:S(2)}, u32[]{:S(2)}) collective-permute-start(f32[2,40,1536]{2,1,0:T(8,128)} %get-tuple-element.11), channel_id=1, source_target_pairs={{0,16},{8,24},{16,32},{24,40},{32,48},{40,56},{48,0},{56,8},{64,80... | collective-permute-start | bytes 1474568 | tf_op jit(solution)/shard_map/ppermute | solution.py:17
  83.5 47.7 %collective-permute-start.2 = (f32[2,40,1536]{2,1,0:T(8,128)}, f32[2,40,1536]{2,1,0:T(8,128)}, u32[]{:S(2)}, u32[]{:S(2)}) collective-permute-start(f32[2,40,1536]{2,1,0:T(8,128)} %get-tuple-element.13), channel_id=1, source_target_pairs={{0,32},{8,40},{16,48},{24,56},{32,0},{40,8},{48,16},{56,24},{64,96... | collective-permute-start | bytes 1474568 | tf_op jit(solution)/shard_map/ppermute | solution.py:17
  86.2 45.0 %collective-permute-start.3 = (f32[2,40,1536]{2,1,0:T(8,128)S(1)}, f32[2,40,1536]{2,1,0:T(8,128)}, u32[]{:S(2)}, u32[]{:S(2)}) collective-permute-start(f32[2,40,1536]{2,1,0:T(8,128)S(1)} %get-tuple-element.12), channel_id=1, source_target_pairs={{0,48},{8,56},{16,0},{24,8},{32,16},{40,24},{48,32},{56,40},{64,11... | collective-permute-start | bytes 1474568 | tf_op jit(solution)/shard_map/ppermute | solution.py:17
  117.4 19.6 %collective-permute-start.5 = (f32[2,24,1536]{2,1,0:T(8,128)S(1)}, f32[2,24,1536]{2,1,0:T(8,128)S(1)}, u32[]{:S(2)}, u32[]{:S(2)}) collective-permute-start(f32[2,24,1536]{2,1,0:T(8,128)S(1)} %get-tuple-element.14), channel_id=1, source_target_pairs={{0,16},{8,24},{16,32},{24,40},{32,48},{40,56},{48,0},{56,8},{64,80... | collective-permute-start | bytes 884744 | tf_op jit(solution)/shard_map/ppermute | solution.py:17
  128.5 13.8 %collective-permute-start.6 = (f32[2,24,1536]{2,1,0:T(8,128)S(1)}, f32[2,24,1536]{2,1,0:T(8,128)S(1)}, u32[]{:S(2)}, u32[]{:S(2)}) collective-permute-start(f32[2,24,1536]{2,1,0:T(8,128)S(1)} %get-tuple-element.16), channel_id=1, source_target_pairs={{0,32},{8,40},{16,48},{24,56},{32,0},{40,8},{48,16},{56,24},{64,96... | collective-permute-start | bytes 884744 | tf_op jit(solution)/shard_map/ppermute | solution.py:17
  128.5 13.8 %collective-permute-start.7 = (f32[2,24,1536]{2,1,0:T(8,128)S(1)}, f32[2,24,1536]{2,1,0:T(8,128)S(1)}, u32[]{:S(2)}, u32[]{:S(2)}) collective-permute-start(f32[2,24,1536]{2,1,0:T(8,128)S(1)} %get-tuple-element.15), channel_id=1, source_target_pairs={{0,48},{8,56},{16,0},{24,8},{32,16},{40,24},{48,32},{56,40},{64,11... | collective-permute-start | bytes 884744 | tf_op jit(solution)/shard_map/ppermute | solution.py:17
  132.7 12.7 %collective-permute-start.4 = (f32[40,1536]{1,0:T(8,128)S(1)}, f32[40,1536]{1,0:T(8,128)S(1)}, u32[]{:S(2)}, u32[]{:S(2)}) collective-permute-start(f32[40,1536]{1,0:T(8,128)S(1)} %dynamic-slice_bitcast_fusion.6), channel_id=1, source_target_pairs={{0,64},{8,72},{16,80},{24,88},{32,96},{40,104},{48,112},{56,120},{... | collective-permute-start | bytes 737288 | tf_op jit(solution)/shard_map/ppermute | solution.py:17
  142.3 6.7 %collective-permute-start.8 = (f32[24,1536]{1,0:T(8,128)S(1)}, f32[24,1536]{1,0:T(8,128)S(1)}, u32[]{:S(2)}, u32[]{:S(2)}) collective-permute-start(f32[24,1536]{1,0:T(8,128)S(1)} %dynamic-slice_bitcast_fusion.7), channel_id=1, source_target_pairs={{0,64},{8,72},{16,80},{24,88},{32,96},{40,104},{48,112},{56,120},{... | collective-permute-start | bytes 442376 | tf_op jit(solution)/shard_map/ppermute | solution.py:17
  149.1 13.4 %copy-start = (f32[64,192]{1,0:T(8,128)S(1)}, f32[64,192]{1,0:T(8,128)}, u32[]{:S(2)}) copy-start(f32[64,192]{1,0:T(8,128)} %param.8) | copy-start | bytes 147460
  149.1 13.4 %copy-start.1 = (f32[64,192]{1,0:T(8,128)S(1)}, f32[64,192]{1,0:T(8,128)}, u32[]{:S(2)}) copy-start(f32[64,192]{1,0:T(8,128)} %param.9) | copy-start | bytes 147460
  149.1 13.4 %copy-start.2 = (f32[192]{0:T(256)S(1)}, f32[192]{0:T(256)}, u32[]{:S(2)}) copy-start(f32[192]{0:T(256)} %param.11) | copy-start | bytes 2308
  149.2 13.4 %copy-start.3 = (f32[64]{0:T(128)S(1)}, f32[64]{0:T(128)}, u32[]{:S(2)}) copy-start(f32[64]{0:T(128)} %param.10) | copy-start | bytes 772
